TPU v7x, 32 devices: a whole 2x2x4 slice. The times are simulated.
32 devices in a mesh: seq: 16 (over z, y, x), grp: 2 (over core).
Axes of the slice: x: 2, y: 2, z: 4, core: 2. Of those that a mesh axis runs over, the one named last changes fastest.
Arguments:
- queries: bfloat16 [4096, 2048], P('seq', 'grp'), parts along dimension 1, may hold values from -80 to 80
- shared_keys: bfloat16 [4096, 256], P('seq', 'grp'), parts along dimension 1, may hold values from -4 to 4
- shared_values: bfloat16 [4096, 256], P('seq', 'grp'), parts along dimension 1, may hold values from -6 to 6
- outputs: bfloat16 [4096, 2048], P('seq', 'grp'), parts along dimension 1, may hold values from -6 to 6
- out_grad: bfloat16 [4096, 2048], P('seq', 'grp'), parts along dimension 1, may hold values from -6 to 6
- doc_lengths: int32 [64], replicated, may hold values from 1 to 2048, 4096 in all
Outputs:
- grad_queries: bfloat16 [4096, 2048], P('seq', 'grp'), parts along dimension 1
- grad_keys: bfloat16 [4096, 256], P('seq', 'grp'), parts along dimension 1
- grad_values: bfloat16 [4096, 256], P('seq', 'grp'), parts along dimension 1
There are 2 independent parts, one for each index of `grp`. A program takes and returns all parts, laid end to end along the dimension named above; an argument that names none is the same for every part. Nothing has to cross between parts.
Inputs may be any that keep to these rules, and one draw needn't show every extreme that they name: `doc_lengths`: lengths of the 64 documents in packing order; they sum to 4096 and the longest is exactly 2048.
All inputs are finite; a program needn't handle non-finite values.
Results may differ from a plain program's by a relative error of at most 0.0051.
Values may be sent and summed in bfloat16 or wider, within the bound.
No kernel may reach another device: no remote copies, remote signals or barrier semaphores. Data moves between devices by JAX's collectives and lax.ppermute only.
A program may use at most 64 MiB of HBM per device.

v0:
```python
import functools

import jax
import jax.numpy as jnp
from jax import lax
from jax.experimental import pallas as pl
from jax.experimental.pallas import tpu as pltpu
from jax.sharding import PartitionSpec as P

REACH = 16


def _bwd_kernel(blk_ref, starts_ref, srow_ref, dst_ref, q_ref, do_ref, kv_hbm,
                delta_ref, dq_ref, part_ref, qall, doall, dqt, kvbuf, sems, sbuf, dsbuf,
                *, rows, heads, width, reach, scaling, docs):
    s = pl.program_id(0)
    win = reach + 1

    def copy(side, i):
        row = pl.multiple_of(srow_ref[side * win + i], rows)
        return pltpu.make_async_copy(
            kv_hbm.at[pl.ds(row, rows)], kvbuf.at[side, i], sems.at[side, i]
        )

    @pl.when(s == 0)
    def _():
        for side in range(2):
            for i in range(win):
                copy(side, i).start()
        part_ref[...] = jnp.zeros(part_ref.shape, jnp.float32)

    b = blk_ref[s]
    cols = heads * rows
    qpos = b * rows + lax.broadcasted_iota(jnp.int32, (1, cols), 1) % rows
    first = b * rows

    def doc_step(j, carry):
        vec, low = carry
        st = starts_ref[j]
        vec = jnp.where(st <= qpos, jnp.maximum(vec, st), vec)
        low = jnp.where(st <= first, jnp.maximum(low, st), low)
        return vec, low

    begin, low = lax.fori_loop(
        0, docs, doc_step, (jnp.zeros((1, cols), jnp.int32), jnp.int32(0))
    )
    kb0 = jnp.maximum(0, low // rows - (b - reach))
    for h in range(heads):
        qall[h * rows:(h + 1) * rows, :] = q_ref[:, h * width:(h + 1) * width]
        doall[h * rows:(h + 1) * rows, :] = do_ref[:, h * width:(h + 1) * width]
    delta = delta_ref[...]
    k_iota = lax.broadcasted_iota(jnp.int32, (rows, 1), 0)
    base = (b - reach) * rows
    nt = (((1,), (1,)), ((), ()))
    tn = (((0,), (0,)), ((), ()))
    for i in range(win):
        copy(s, i).wait()

    def scores(c):
        kc = kvbuf[s, c, :, :width]
        st = lax.dot_general(kc, qall[...], nt, preferred_element_type=jnp.float32) * scaling
        kpos = base + c * rows + k_iota
        allowed = (kpos >= begin) & (kpos <= qpos)
        return kc, st, allowed

    def stat_step(c, m):
        _, st, allowed = scores(c)
        masked = jnp.where(allowed, st, -1e30)
        sbuf[c] = masked
        return jnp.maximum(m, jnp.max(masked, axis=0, keepdims=True))

    m0 = jnp.full((1, cols), -1e30, jnp.float32)
    l0 = jnp.zeros((1, cols), jnp.float32)
    m = lax.fori_loop(kb0, win, stat_step, m0)

    def exp_step(c, l):
        e = jnp.exp(sbuf[c] - m)
        sbuf[c] = e
        return l + jnp.sum(e, axis=0, keepdims=True)

    inv_l = 1.0 / lax.fori_loop(kb0, win, exp_step, l0)

    def grad_step(c, carry):
        p = sbuf[c] * inv_l
        vc = kvbuf[s, c, :, width:]
        dpt = lax.dot_general(vc, doall[...], nt, preferred_element_type=jnp.float32)
        ds = (p * (dpt - delta)).astype(jnp.bfloat16)
        pb = p.astype(jnp.bfloat16)
        dk = jnp.dot(ds, qall[...], preferred_element_type=jnp.float32) * scaling
        dv = jnp.dot(pb, doall[...], preferred_element_type=jnp.float32)
        dst = dst_ref[s * win + c]
        part_ref[dst, :, :width] += dk
        part_ref[dst, :, width:] += dv
        dsbuf[c] = ds
        return carry

    lax.fori_loop(kb0, win, grad_step, 0)

    def clear_step(c, carry):
        dsbuf[c] = jnp.zeros((rows, cols), jnp.bfloat16)
        return carry

    lax.fori_loop(0, kb0, clear_step, 0)
    kwin = kvbuf[s, :, :, :width].reshape(win * rows, width)
    dqt[...] = lax.dot_general(
        kwin, dsbuf[...].reshape(win * rows, cols), tn, preferred_element_type=jnp.float32
    )
    for h in range(heads):
        piece = dqt[:, h * rows:(h + 1) * rows]
        dq_ref[:, h * width:(h + 1) * width] = (piece.T * scaling).astype(jnp.bfloat16)


def _shift(x, k, n, axis):
    return lax.ppermute(x, axis, [(i, (i + k) % n) for i in range(n)])


def _group_gather(x, n, axis):
    return jnp.stack([x] + [_shift(x, k, n, axis) for k in range(1, n)])


def _group_reduce(parts, n, axis, dim):
    me = lax.axis_index(axis)
    total = lax.dynamic_index_in_dim(parts, me, dim, keepdims=False).astype(jnp.float32)
    for k in range(1, n):
        piece = lax.dynamic_index_in_dim(parts, (me + k) % n, dim, keepdims=False)
        total = total + _shift(piece.astype(jnp.bfloat16), k, n, axis).astype(jnp.float32)
    return total


def body(queries, shared_keys, shared_values, outputs, out_grad, doc_lengths):
    n_in = lax.axis_size("w")
    rank = lax.axis_index("zp") * n_in + lax.axis_index("w")
    n_out = lax.axis_size("zp")
    n_seq = n_out * n_in
    rows = shared_keys.shape[0] // 2
    width = shared_keys.shape[1]
    heads = queries.shape[1] // width
    scaling = width ** (-0.5)
    win = REACH + 1
    doc_ends = jnp.cumsum(doc_lengths)
    doc_starts = doc_ends - doc_lengths
    blocks = jnp.stack([rank, 2 * n_seq - 1 - rank]).astype(jnp.int32)

    kv_local = jnp.concatenate([shared_keys, shared_values], axis=1)
    kv_col = _group_gather(kv_local, n_out, "zp")
    kv_recv = _group_gather(kv_col, n_in, "w").reshape(n_in * n_out * 2 * rows, 2 * width)

    me_z = lax.axis_index("zp")
    me_w = lax.axis_index("w")
    seq_blk = (blocks[:, None] - REACH + jnp.arange(win, dtype=jnp.int32)[None, :]).reshape(-1)
    seq_blk = jnp.maximum(seq_blk, 0)
    dev = jnp.where(seq_blk < n_seq, seq_blk, 2 * n_seq - 1 - seq_blk)
    slot = (seq_blk >= n_seq).astype(jnp.int32)
    k_z = (me_z - dev // n_in) % n_out
    k_w = (me_w - dev % n_in) % n_in
    srow = (((k_w * n_out + k_z) * 2 + slot) * rows).astype(jnp.int32)
    dst = (dev * 2 + slot).astype(jnp.int32)

    prod = out_grad.astype(jnp.float32) * outputs.astype(jnp.float32)
    deltas = jnp.sum(prod.reshape(2, rows, heads, width), axis=3)
    delta_t = jnp.swapaxes(deltas, 1, 2).reshape(2, 1, heads * rows)

    kernel = functools.partial(
        _bwd_kernel, rows=rows, heads=heads, width=width, reach=REACH, scaling=scaling,
        docs=doc_lengths.shape[0],
    )
    cols = heads * rows
    vec = pl.BlockSpec((None, 1, cols), lambda s, *_: (s, 0, 0))
    grid_spec = pltpu.PrefetchScalarGridSpec(
        num_scalar_prefetch=4,
        grid=(2,),
        in_specs=[
            pl.BlockSpec((rows, cols), lambda s, *_: (s, 0)),
            pl.BlockSpec((rows, cols), lambda s, *_: (s, 0)),
            pl.BlockSpec(memory_space=pl.ANY),
            vec,
        ],
        out_specs=[
            pl.BlockSpec((rows, cols), lambda s, *_: (s, 0)),
            pl.BlockSpec((2 * n_seq, rows, 2 * width), lambda s, *_: (0, 0, 0)),
        ],
        scratch_shapes=[
            pltpu.VMEM((cols, width), jnp.bfloat16),
            pltpu.VMEM((cols, width), jnp.bfloat16),
            pltpu.VMEM((width, cols), jnp.float32),
            pltpu.VMEM((2, win, rows, 2 * width), jnp.bfloat16),
            pltpu.SemaphoreType.DMA((2, win)),
            pltpu.VMEM((win, rows, cols), jnp.float32),
            pltpu.VMEM((win, rows, cols), jnp.bfloat16),
        ],
    )
    flops = 2 * 2 * win * 6 * rows * cols * width
    grad_queries, partial = pl.pallas_call(
        kernel,
        grid_spec=grid_spec,
        out_shape=[
            jax.ShapeDtypeStruct((2 * rows, cols), jnp.bfloat16),
            jax.ShapeDtypeStruct((2 * n_seq, rows, 2 * width), jnp.float32),
        ],
        compiler_params=pltpu.CompilerParams(dimension_semantics=("arbitrary",)),
        cost_estimate=pl.CostEstimate(
            flops=flops, transcendentals=2 * 2 * win * rows * cols, bytes_accessed=8 << 20
        ),
    )(blocks, doc_starts.astype(jnp.int32), srow, dst, queries, out_grad, kv_recv, delta_t)

    storage = partial
    storage = storage.reshape(n_out, n_in, 2, rows, 2 * width)
    plane = _group_reduce(storage, n_in, "w", 1)
    summed = _group_reduce(plane, n_out, "zp", 0).reshape(2 * rows, 2 * width)
    grad_keys = summed[:, :width].astype(jnp.bfloat16)
    grad_values = summed[:, width:].astype(jnp.bfloat16)
    return (grad_queries, grad_keys, grad_values)


GROUP = 4


def solution(mesh):
    n_seq, n_grp = mesh.devices.shape
    split = mesh.devices.reshape(n_seq // GROUP, GROUP, n_grp)
    mesh2 = jax.sharding.Mesh(split, ("zp", "w", "grp"))
    rows = P(("zp", "w"), "grp")
    placed = (rows, rows, rows, rows, rows, P())
    return jax.shard_map(
        body,
        mesh=mesh2,
        in_specs=placed,
        out_specs=(rows, rows, rows),
        check_vma=False,
    )
```

profile of v0, /device:TPU:0, one launch (start us, length us, event | category | flops | bytes accessed | tf_op | source)
XLA Modules:
  0.0 112.3 jit_solution(7601170202314970618)
XLA Ops:
  0.6 0.0 copy-start.1
  0.7 0.9 constant_dynamic-update-slice_fusion.1
  1.6 0.9 constant_dynamic-update-slice_fusion
  2.5 5.1 %collective-permute-start.2 = (bf16[256,256]{1,0:T(8,128)(2,1)S(1)}, bf16[256,256]{1,0:T(8,128)(2,1)S(1)}, u32[]{:S(2)}, u32[]{:S(2)}) collective-permute-start(bf16[256,256]{1,0:T(8,128)(2,1)S(1)} %constant_dynamic-update-slice_fusion), channel_id=1, source_target_pairs={{0,24},{8,0},{16,8},{24,16},{1,25},{9,1},{17,9},{25,17},{2,26},{10... | collective-permute-start | bytes 393224 | tf_op jit(solution)/shard_map/ppermute | solution.py:114
  7.6 0.0 collective-permute-start.1
  7.6 1.0 collective-permute-start
  8.6 0.7 copy.15
  9.3 0.1 reduce-window.9
  9.4 0.1 reduce
  9.5 1.3 %sub.34.starts_ref = s32[64]{0:T(128)} subtract(s32[64]{0:T(128)S(1)} %reduce, s32[64]{0:T(128)} %param.11) | non-fusion elementwise | flops 64 | bytes 768 | tf_op jit(solution)/shard_map/sub | solution.py:141
  10.8 0.7 broadcast_add_fusion
  11.5 0.1 add_maximum_fusion
  11.5 0.1 max.13
  11.6 0.0 collective-permute-done.2
  11.6 7.2 %collective-permute-done.1 = bf16[256,256]{1,0:T(8,128)(2,1)S(1)} collective-permute-done((bf16[256,256]{1,0:T(8,128)(2,1)S(1)}, bf16[256,256]{1,0:T(8,128)(2,1)S(1)}, u32[]{:S(2)}, u32[]{:S(2)}) %collective-permute-start.1) | collective-permute-done | bytes 131104 | tf_op jit(solution)/shard_map/ppermute | solution.py:114
  18.8 0.0 collective-permute-done
  18.8 0.1 fusion.16
  18.9 2.5 %collective-permute-start.5 = (bf16[4,256,256]{2,1,0:T(8,128)(2,1)S(1)}, bf16[4,256,256]{2,1,0:T(8,128)(2,1)S(1)}, u32[]{:S(2)}, u32[]{:S(2)}) collective-permute-start(bf16[4,256,256]{2,1,0:T(8,128)(2,1)S(1)} %get-tuple-element.16), channel_id=1, source_target_pairs={{0,6},{2,0},{4,2},{6,4},{1,7},{3,1},{5,3},{7,5},{8,14},{10,8},{12,... | collective-permute-start | bytes 1572872 | tf_op jit(solution)/shard_map/ppermute | solution.py:114
  21.4 0.5 collective-permute-start.4
  21.9 0.6 collective-permute-start.3
  22.5 0.0 copy-done.1
  22.5 0.2 multiply_bitcast_fusion
  22.7 0.2 copy.21
  22.9 0.3 bitcast_reduce_fusion
  23.2 0.7 copy.16
  23.9 0.5 multiply_add_fusion
  24.4 9.3 %collective-permute-done.5 = bf16[4,256,256]{2,1,0:T(8,128)(2,1)S(1)} collective-permute-done((bf16[4,256,256]{2,1,0:T(8,128)(2,1)S(1)}, bf16[4,256,256]{2,1,0:T(8,128)(2,1)S(1)}, u32[]{:S(2)}, u32[]{:S(2)}) %collective-permute-start.5) | collective-permute-done | bytes 524320 | tf_op jit(solution)/shard_map/ppermute | solution.py:114
  33.7 11.8 %collective-permute-done.4 = bf16[4,256,256]{2,1,0:T(8,128)(2,1)S(1)} collective-permute-done((bf16[4,256,256]{2,1,0:T(8,128)(2,1)S(1)}, bf16[4,256,256]{2,1,0:T(8,128)(2,1)S(1)}, u32[]{:S(2)}, u32[]{:S(2)}) %collective-permute-start.4) | collective-permute-done | bytes 524320 | tf_op jit(solution)/shard_map/ppermute | solution.py:114
  45.6 0.0 collective-permute-done.3
  45.6 2.6 %pad_maximum_fusion = bf16[4,4,256,256]{3,2,1,0:T(8,128)(2,1)} fusion(bf16[1,4,256,256]{3,2,1,0:T(8,128)(2,1)S(1)} %bitcast.63, bf16[1,4,256,256]{3,2,1,0:T(8,128)(2,1)S(1)} %bitcast.64, bf16[1,4,256,256]{3,2,1,0:T(8,128)(2,1)} %bitcast.8, bf16[1,4,256,256]{3,2,1,0:T(8,128)(2,1)S(1)} %get-tuple-element.15), kind=kLoop, calls=%fused_computation | loop fusion | flops 3145728 | bytes 4194304 | tf_op jit(solution)/shard_map/stack | solution.py:118
  48.2 13.4 %shard_map.85 = (bf16[256,1024]{1,0:T(8,128)(2,1)}, f32[32,128,256]{2,1,0:T(8,128)}) custom-call(s32[2]{0:T(128)} %get-tuple-element.8.blk_ref, s32[64]{0:T(128)} %sub.34.starts_ref, s32[34]{0:T(128)} %get-tuple-element.20.srow_ref, s32[34]{0:T(128)} %get-tuple-element.19.dst_ref, bf16[256,1024]{1,0:T(8,128)(2,1)} %q_ref.1, bf16[256,1024]{1,0:T(8,128)(2,1)} %do_ref.1, ...), custom_call_target="tpu_custom_call" | custom-call | flops 6845104128 | bytes 8388608 | tf_op jit(solution)/shard_map/pallas_call | solution.py:193
  61.6 2.1 %fusion.3 = (bf16[4,2,128,256]{3,2,1,0:T(8,128)(2,1)S(1)}, bf16[4,2,128,256]{3,2,1,0:T(8,128)(2,1)S(1)}, bf16[4,2,128,256]{3,2,1,0:T(8,128)(2,1)S(1)}) fusion(f32[4,4,2,128,256]{4,3,2,1,0:T(8,128)} %bitcast.59, s32[]{:T(128)S(6)} %select_n.82, s32[]{:T(128)S(6)} %select_n.86, s32[]{:T(128)S(6)} %select_n.84), kind=kLoop, calls=%fused_computation.10 | loop fusion | bytes 3145740 | tf_op jit(solution)/shard_map/convert_element_type | solution.py:126
  63.7 0.1 collective-permute-start.8
  63.8 1.8 %collective-permute-start.7 = (bf16[4,2,128,256]{3,2,1,0:T(8,128)(2,1)S(1)}, bf16[4,2,128,256]{3,2,1,0:T(8,128)(2,1)S(1)}, u32[]{:S(2)}, u32[]{:S(2)}) collective-permute-start(bf16[4,2,128,256]{3,2,1,0:T(8,128)(2,1)S(1)} %get-tuple-element.11), channel_id=1, source_target_pairs={{0,4},{2,6},{4,0},{6,2},{1,5},{3,7},{5,1},{7,3},{8,12},{10,14},{12... | collective-permute-start | bytes 1572872 | tf_op jit(solution)/shard_map/ppermute | solution.py:114
  65.6 0.3 collective-permute-start.6
  65.9 12.6 %collective-permute-done.8 = bf16[4,2,128,256]{3,2,1,0:T(8,128)(2,1)S(1)} collective-permute-done((bf16[4,2,128,256]{3,2,1,0:T(8,128)(2,1)S(1)}, bf16[4,2,128,256]{3,2,1,0:T(8,128)(2,1)S(1)}, u32[]{:S(2)}, u32[]{:S(2)}) %collective-permute-start.8) | collective-permute-done | bytes 524320 | tf_op jit(solution)/shard_map/ppermute | solution.py:114
  78.5 8.7 %collective-permute-done.7 = bf16[4,2,128,256]{3,2,1,0:T(8,128)(2,1)S(1)} collective-permute-done((bf16[4,2,128,256]{3,2,1,0:T(8,128)(2,1)S(1)}, bf16[4,2,128,256]{3,2,1,0:T(8,128)(2,1)S(1)}, u32[]{:S(2)}, u32[]{:S(2)}) %collective-permute-start.7) | collective-permute-done | bytes 524320 | tf_op jit(solution)/shard_map/ppermute | solution.py:114
  87.2 0.0 collective-permute-done.6
  87.2 1.4 %fusion.1 = f32[4,2,128,256]{3,2,1,0:T(8,128)S(1)} fusion(bf16[4,2,128,256]{3,2,1,0:T(8,128)(2,1)S(1)} %collective-permute-done.8, bf16[4,2,128,256]{3,2,1,0:T(8,128)(2,1)S(1)} %collective-permute-done.7, bf16[4,2,128,256]{3,2,1,0:T(8,128)(2,1)S(1)} %collective-permute-done.6, f32[4,4,2,128,256]{4,3,2,1,0:T(8,128)} %bitcast.60, s32[]{:T(128)S(6)} %select_n.80), kind=kLoop, calls=%fused_computation.6 | loop fusion | flops 1572864 | bytes 3670020 | tf_op jit(solution)/shard_map/add | solution.py:126
  88.7 0.1 fusion.8
  88.7 9.6 %collective-permute-start.11 = (bf16[2,128,256]{2,1,0:T(8,128)(2,1)S(1)}, bf16[2,128,256]{2,1,0:T(8,128)(2,1)S(1)}, u32[]{:S(2)}, u32[]{:S(2)}) collective-permute-start(bf16[2,128,256]{2,1,0:T(8,128)(2,1)S(1)} %get-tuple-element.13), channel_id=1, source_target_pairs={{0,24},{8,0},{16,8},{24,16},{1,25},{9,1},{17,9},{25,17},{2,26},{10... | collective-permute-start | bytes 393224 | tf_op jit(solution)/shard_map/ppermute | solution.py:114
  98.4 3.9 %collective-permute-start.10 = (bf16[2,128,256]{2,1,0:T(8,128)(2,1)S(1)}, bf16[2,128,256]{2,1,0:T(8,128)(2,1)S(1)}, u32[]{:S(2)}, u32[]{:S(2)}) collective-permute-start(bf16[2,128,256]{2,1,0:T(8,128)(2,1)S(1)} %get-tuple-element.14), channel_id=1, source_target_pairs={{0,16},{8,24},{16,0},{24,8},{1,17},{9,25},{17,1},{25,9},{2,18},{10... | collective-permute-start | bytes 393224 | tf_op jit(solution)/shard_map/ppermute | solution.py:114
  102.2 0.6 collective-permute-start.9
  102.8 3.4 %collective-permute-done.11 = bf16[2,128,256]{2,1,0:T(8,128)(2,1)S(1)} collective-permute-done((bf16[2,128,256]{2,1,0:T(8,128)(2,1)S(1)}, bf16[2,128,256]{2,1,0:T(8,128)(2,1)S(1)}, u32[]{:S(2)}, u32[]{:S(2)}) %collective-permute-start.11) | collective-permute-done | bytes 131104 | tf_op jit(solution)/shard_map/ppermute | solution.py:114
  106.3 5.3 %collective-permute-done.10 = bf16[2,128,256]{2,1,0:T(8,128)(2,1)S(1)} collective-permute-done((bf16[2,128,256]{2,1,0:T(8,128)(2,1)S(1)}, bf16[2,128,256]{2,1,0:T(8,128)(2,1)S(1)}, u32[]{:S(2)}, u32[]{:S(2)}) %collective-permute-start.10) | collective-permute-done | bytes 131104 | tf_op jit(solution)/shard_map/ppermute | solution.py:114
  111.6 0.0 collective-permute-done.9
  111.6 0.1 fusion.7
  111.6 0.7 fusion.17
  (2 shorter events, 0.0 us)
Async XLA Ops:
  0.6 21.9 %copy-start.1 = (bf16[256,1024]{1,0:T(8,128)(2,1)S(1)}, bf16[256,1024]{1,0:T(8,128)(2,1)}, u32[]{:S(2)}) copy-start(bf16[256,1024]{1,0:T(8,128)(2,1)} %do_ref.1) | copy-start | bytes 1572868
  0.6 21.9 %copy-start = (bf16[256,1024]{1,0:T(8,128)(2,1)S(1)}, bf16[256,1024]{1,0:T(8,128)(2,1)}, u32[]{:S(2)}) copy-start(bf16[256,1024]{1,0:T(8,128)(2,1)} %param.9) | copy-start | bytes 1572868
  2.5 9.2 %collective-permute-start.2 = (bf16[256,256]{1,0:T(8,128)(2,1)S(1)}, bf16[256,256]{1,0:T(8,128)(2,1)S(1)}, u32[]{:S(2)}, u32[]{:S(2)}) collective-permute-start(bf16[256,256]{1,0:T(8,128)(2,1)S(1)} %constant_dynamic-update-slice_fusion), channel_id=1, source_target_pairs={{0,24},{8,0},{16,8},{24,16},{1,25},{9,1},{17,9},{25,17},{2,26},{10... | collective-permute-start | bytes 393224 | tf_op jit(solution)/shard_map/ppermute | solution.py:114
  7.6 11.2 %collective-permute-start.1 = (bf16[256,256]{1,0:T(8,128)(2,1)S(1)}, bf16[256,256]{1,0:T(8,128)(2,1)S(1)}, u32[]{:S(2)}, u32[]{:S(2)}) collective-permute-start(bf16[256,256]{1,0:T(8,128)(2,1)S(1)} %constant_dynamic-update-slice_fusion), channel_id=1, source_target_pairs={{0,16},{8,24},{16,0},{24,8},{1,17},{9,25},{17,1},{25,9},{2,18},{10... | collective-permute-start | bytes 393224 | tf_op jit(solution)/shard_map/ppermute | solution.py:114
  7.6 11.2 %collective-permute-start = (bf16[256,256]{1,0:T(8,128)(2,1)S(1)}, bf16[256,256]{1,0:T(8,128)(2,1)S(1)}, u32[]{:S(2)}, u32[]{:S(2)}) collective-permute-start(bf16[256,256]{1,0:T(8,128)(2,1)S(1)} %constant_dynamic-update-slice_fusion), channel_id=1, source_target_pairs={{0,8},{8,16},{16,24},{24,0},{1,9},{9,17},{17,25},{25,1},{2,10},{10... | collective-permute-start | bytes 393224 | tf_op jit(solution)/shard_map/ppermute | solution.py:114
  18.9 14.8 %collective-permute-start.5 = (bf16[4,256,256]{2,1,0:T(8,128)(2,1)S(1)}, bf16[4,256,256]{2,1,0:T(8,128)(2,1)S(1)}, u32[]{:S(2)}, u32[]{:S(2)}) collective-permute-start(bf16[4,256,256]{2,1,0:T(8,128)(2,1)S(1)} %get-tuple-element.16), channel_id=1, source_target_pairs={{0,6},{2,0},{4,2},{6,4},{1,7},{3,1},{5,3},{7,5},{8,14},{10,8},{12,... | collective-permute-start | bytes 1572872 | tf_op jit(solution)/shard_map/ppermute | solution.py:114
  21.4 24.2 %collective-permute-start.4 = (bf16[4,256,256]{2,1,0:T(8,128)(2,1)S(1)}, bf16[4,256,256]{2,1,0:T(8,128)(2,1)S(1)}, u32[]{:S(2)}, u32[]{:S(2)}) collective-permute-start(bf16[4,256,256]{2,1,0:T(8,128)(2,1)S(1)} %get-tuple-element.16), channel_id=1, source_target_pairs={{0,4},{2,6},{4,0},{6,2},{1,5},{3,7},{5,1},{7,3},{8,12},{10,14},{12... | collective-permute-start | bytes 1572872 | tf_op jit(solution)/shard_map/ppermute | solution.py:114
  21.9 23.7 %collective-permute-start.3 = (bf16[4,256,256]{2,1,0:T(8,128)(2,1)S(1)}, bf16[4,256,256]{2,1,0:T(8,128)(2,1)}, u32[]{:S(2)}, u32[]{:S(2)}) collective-permute-start(bf16[4,256,256]{2,1,0:T(8,128)(2,1)S(1)} %get-tuple-element.16), channel_id=1, source_target_pairs={{0,2},{2,4},{4,6},{6,0},{1,3},{3,5},{5,7},{7,1},{8,10},{10,12},{12... | collective-permute-start | bytes 1572872 | tf_op jit(solution)/shard_map/ppermute | solution.py:114
  63.7 14.8 %collective-permute-start.8 = (bf16[4,2,128,256]{3,2,1,0:T(8,128)(2,1)S(1)}, bf16[4,2,128,256]{3,2,1,0:T(8,128)(2,1)S(1)}, u32[]{:S(2)}, u32[]{:S(2)}) collective-permute-start(bf16[4,2,128,256]{3,2,1,0:T(8,128)(2,1)S(1)} %get-tuple-element.10), channel_id=1, source_target_pairs={{0,6},{2,0},{4,2},{6,4},{1,7},{3,1},{5,3},{7,5},{8,14},{10,8},{12,... | collective-permute-start | bytes 1572872 | tf_op jit(solution)/shard_map/ppermute | solution.py:114
  63.8 23.5 %collective-permute-start.7 = (bf16[4,2,128,256]{3,2,1,0:T(8,128)(2,1)S(1)}, bf16[4,2,128,256]{3,2,1,0:T(8,128)(2,1)S(1)}, u32[]{:S(2)}, u32[]{:S(2)}) collective-permute-start(bf16[4,2,128,256]{3,2,1,0:T(8,128)(2,1)S(1)} %get-tuple-element.11), channel_id=1, source_target_pairs={{0,4},{2,6},{4,0},{6,2},{1,5},{3,7},{5,1},{7,3},{8,12},{10,14},{12... | collective-permute-start | bytes 1572872 | tf_op jit(solution)/shard_map/ppermute | solution.py:114
  65.6 21.7 %collective-permute-start.6 = (bf16[4,2,128,256]{3,2,1,0:T(8,128)(2,1)S(1)}, bf16[4,2,128,256]{3,2,1,0:T(8,128)(2,1)S(1)}, u32[]{:S(2)}, u32[]{:S(2)}) collective-permute-start(bf16[4,2,128,256]{3,2,1,0:T(8,128)(2,1)S(1)} %get-tuple-element.9), channel_id=1, source_target_pairs={{0,2},{2,4},{4,6},{6,0},{1,3},{3,5},{5,7},{7,1},{8,10},{10,12},{12... | collective-permute-start | bytes 1572872 | tf_op jit(solution)/shard_map/ppermute | solution.py:114
  88.7 17.5 %collective-permute-start.11 = (bf16[2,128,256]{2,1,0:T(8,128)(2,1)S(1)}, bf16[2,128,256]{2,1,0:T(8,128)(2,1)S(1)}, u32[]{:S(2)}, u32[]{:S(2)}) collective-permute-start(bf16[2,128,256]{2,1,0:T(8,128)(2,1)S(1)} %get-tuple-element.13), channel_id=1, source_target_pairs={{0,24},{8,0},{16,8},{24,16},{1,25},{9,1},{17,9},{25,17},{2,26},{10... | collective-permute-start | bytes 393224 | tf_op jit(solution)/shard_map/ppermute | solution.py:114
  98.4 13.2 %collective-permute-start.10 = (bf16[2,128,256]{2,1,0:T(8,128)(2,1)S(1)}, bf16[2,128,256]{2,1,0:T(8,128)(2,1)S(1)}, u32[]{:S(2)}, u32[]{:S(2)}) collective-permute-start(bf16[2,128,256]{2,1,0:T(8,128)(2,1)S(1)} %get-tuple-element.14), channel_id=1, source_target_pairs={{0,16},{8,24},{16,0},{24,8},{1,17},{9,25},{17,1},{25,9},{2,18},{10... | collective-permute-start | bytes 393224 | tf_op jit(solution)/shard_map/ppermute | solution.py:114
  102.2 9.3 %collective-permute-start.9 = (bf16[2,128,256]{2,1,0:T(8,128)(2,1)S(1)}, bf16[2,128,256]{2,1,0:T(8,128)(2,1)S(1)}, u32[]{:S(2)}, u32[]{:S(2)}) collective-permute-start(bf16[2,128,256]{2,1,0:T(8,128)(2,1)S(1)} %get-tuple-element.12), channel_id=1, source_target_pairs={{0,8},{8,16},{16,24},{24,0},{1,9},{9,17},{17,25},{25,1},{2,10},{10... | collective-permute-start | bytes 393224 | tf_op jit(solution)/shard_map/ppermute | solution.py:114
where the time goes:
time: 112 us
  waiting for transfers between devices  58.4 us (52%)
  starting transfers between devices  26 us (23%)
  Pallas kernels  13.4 us (12%)
  other arithmetic  7.44 us (7%)
  local copies, waits for them, and re-layouts  6.3 us (6%)
    ppermute x12, waiting for transfers between devices, _shift(): return lax.ppermute(x, axis, [(i, (i + k) % n) for i in range(n)])  58.4 us
    ppermute x12, starting transfers between devices, _shift(): return lax.ppermute(x, axis, [(i, (i + k) % n) for i in range(n)])  26 us
    pallas_call x1, Pallas kernels, body(): pl.pallas_call(kernel, grid_spec=grid_spec, out_shape=[jax.ShapeDtypeStru...  13.4 us
    another operation x2, other arithmetic, _group_gather(): return jnp.stack([x] + [_shift(x, k, n, axis) for k in range(1, n)])  2.71 us
  transfers between devices with their start and end apart: 12, of which 7 were waited for; matrix products, arithmetic and copies ran while one was open for 4% of the time, Pallas kernels for 0%

commit v1 on v0

--- a/solution.py
+++ b/solution.py
@@ -12,9 +12,10 @@
 
 def _bwd_kernel(blk_ref, starts_ref, srow_ref, dst_ref, q_ref, do_ref, kv_hbm,
                 delta_ref, dq_ref, part_ref, qall, doall, dqt, kvbuf, sems, sbuf, dsbuf,
-                *, rows, heads, width, reach, scaling, docs):
+                bounds, *, rows, heads, width, reach, scaling, docs, n_seq):
     s = pl.program_id(0)
     win = reach + 1
+    cols = heads * rows
 
     def copy(side, i):
         row = pl.multiple_of(srow_ref[side * win + i], rows)
@@ -22,29 +23,60 @@
             kv_hbm.at[pl.ds(row, rows)], kvbuf.at[side, i], sems.at[side, i]
         )
 
+    def seq_of(d):
+        dev = d // 2
+        return jnp.where(d % 2 == 0, dev, 2 * n_seq - 1 - dev)
+
+    def touched(side, j):
+        top = blk_ref[side]
+        return (j >= top - reach + bounds[2 * side]) & (j <= top)
+
     @pl.when(s == 0)
     def _():
         for side in range(2):
             for i in range(win):
                 copy(side, i).start()
-        part_ref[...] = jnp.zeros(part_ref.shape, jnp.float32)
+
+        def bound_step(j, carry):
+            st = starts_ref[j]
+            out = []
+            for side in range(2):
+                first = blk_ref[side] * rows
+                lo, hi = carry[2 * side], carry[2 * side + 1]
+                out.append(jnp.where(st <= first, jnp.maximum(lo, st), lo))
+                out.append(jnp.where(st <= first + rows - 1, jnp.maximum(hi, st), hi))
+            return tuple(out)
+
+        found = lax.fori_loop(0, docs, bound_step, (jnp.int32(0),) * 4)
+        for side in range(2):
+            top = blk_ref[side]
+            base_side = (top - reach) * rows
+            kb0_side = jnp.maximum(0, found[2 * side] // rows - (top - reach))
+            free = (found[2 * side + 1] - base_side + rows - 1) // rows
+            bounds[2 * side] = kb0_side
+            bounds[2 * side + 1] = jnp.minimum(reach, jnp.maximum(kb0_side, free))
+
+        def zero_step(d, carry):
+            j = seq_of(d)
+
+            @pl.when(jnp.logical_not(touched(0, j) | touched(1, j)))
+            def _():
+                part_ref[d] = jnp.zeros((rows, 2 * width), jnp.float32)
+
+            return carry
+
+        lax.fori_loop(0, 2 * n_seq, zero_step, 0)
 
     b = blk_ref[s]
-    cols = heads * rows
+    kb0 = bounds[2 * s]
+    c_free = bounds[2 * s + 1]
     qpos = b * rows + lax.broadcasted_iota(jnp.int32, (1, cols), 1) % rows
-    first = b * rows
-
-    def doc_step(j, carry):
-        vec, low = carry
+
+    def doc_step(j, vec):
         st = starts_ref[j]
-        vec = jnp.where(st <= qpos, jnp.maximum(vec, st), vec)
-        low = jnp.where(st <= first, jnp.maximum(low, st), low)
-        return vec, low
-
-    begin, low = lax.fori_loop(
-        0, docs, doc_step, (jnp.zeros((1, cols), jnp.int32), jnp.int32(0))
-    )
-    kb0 = jnp.maximum(0, low // rows - (b - reach))
+        return jnp.where(st <= qpos, jnp.maximum(vec, st), vec)
+
+    begin = lax.fori_loop(0, docs, doc_step, jnp.zeros((1, cols), jnp.int32))
     for h in range(heads):
         qall[h * rows:(h + 1) * rows, :] = q_ref[:, h * width:(h + 1) * width]
         doall[h * rows:(h + 1) * rows, :] = do_ref[:, h * width:(h + 1) * width]
@@ -56,22 +88,26 @@
     for i in range(win):
         copy(s, i).wait()
 
-    def scores(c):
+    def stat_masked(c, m):
         kc = kvbuf[s, c, :, :width]
         st = lax.dot_general(kc, qall[...], nt, preferred_element_type=jnp.float32) * scaling
         kpos = base + c * rows + k_iota
         allowed = (kpos >= begin) & (kpos <= qpos)
-        return kc, st, allowed
-
-    def stat_step(c, m):
-        _, st, allowed = scores(c)
         masked = jnp.where(allowed, st, -1e30)
         sbuf[c] = masked
         return jnp.maximum(m, jnp.max(masked, axis=0, keepdims=True))
 
+    def stat_free(c, m):
+        kc = kvbuf[s, c, :, :width]
+        st = lax.dot_general(kc, qall[...], nt, preferred_element_type=jnp.float32) * scaling
+        sbuf[c] = st
+        return jnp.maximum(m, jnp.max(st, axis=0, keepdims=True))
+
     m0 = jnp.full((1, cols), -1e30, jnp.float32)
     l0 = jnp.zeros((1, cols), jnp.float32)
-    m = lax.fori_loop(kb0, win, stat_step, m0)
+    m = lax.fori_loop(kb0, c_free, stat_masked, m0)
+    m = lax.fori_loop(c_free, reach, stat_free, m)
+    m = stat_masked(reach, m)
 
     def exp_step(c, l):
         e = jnp.exp(sbuf[c] - m)
@@ -89,8 +125,18 @@
         dk = jnp.dot(ds, qall[...], preferred_element_type=jnp.float32) * scaling
         dv = jnp.dot(pb, doall[...], preferred_element_type=jnp.float32)
         dst = dst_ref[s * win + c]
-        part_ref[dst, :, :width] += dk
-        part_ref[dst, :, width:] += dv
+        add = (s == 1) & touched(0, b - reach + c)
+
+        @pl.when(add)
+        def _():
+            part_ref[dst, :, :width] += dk
+            part_ref[dst, :, width:] += dv
+
+        @pl.when(jnp.logical_not(add))
+        def _():
+            part_ref[dst, :, :width] = dk
+            part_ref[dst, :, width:] = dv
+
         dsbuf[c] = ds
         return carry
 
@@ -162,7 +208,7 @@
 
     kernel = functools.partial(
         _bwd_kernel, rows=rows, heads=heads, width=width, reach=REACH, scaling=scaling,
-        docs=doc_lengths.shape[0],
+        docs=doc_lengths.shape[0], n_seq=n_seq,
     )
     cols = heads * rows
     vec = pl.BlockSpec((None, 1, cols), lambda s, *_: (s, 0, 0))
@@ -187,6 +233,7 @@
             pltpu.SemaphoreType.DMA((2, win)),
             pltpu.VMEM((win, rows, cols), jnp.float32),
             pltpu.VMEM((win, rows, cols), jnp.bfloat16),
+            pltpu.SMEM((4,), jnp.int32),
         ],
     )
     flops = 2 * 2 * win * 6 * rows * cols * width

time: 112 us -> 118 us (1.054)
  starting transfers between devices: 26 us -> 33.6 us
    ppermute x12, starting transfers between devices: 26 us -> 33.6 us  [_shift(): return lax.ppermute(x, axis, [(i, (i + k) % n) for i in range(n)])]
where the time goes in v1:
time: 118 us; the launch traced here: 119 us
  waiting for transfers between devices  58.1 us (49%)
  starting transfers between devices  33.6 us (28%)
  Pallas kernels  13.3 us (11%)
  other arithmetic  7.44 us (6%)
  local copies, waits for them, and re-layouts  6.3 us (5%)
    ppermute x12, waiting for transfers between devices, _shift(): return lax.ppermute(x, axis, [(i, (i + k) % n) for i in range(n)])  58.1 us
    ppermute x12, starting transfers between devices, _shift(): return lax.ppermute(x, axis, [(i, (i + k) % n) for i in range(n)])  33.6 us
    pallas_call x1, Pallas kernels, body(): pl.pallas_call(kernel, grid_spec=grid_spec, out_shape=[jax.ShapeDtypeStru...  13.3 us
    another operation x2, other arithmetic, _group_gather(): return jnp.stack([x] + [_shift(x, k, n, axis) for k in range(1, n)])  2.71 us
  transfers between devices with their start and end apart: 12, of which 7 were waited for; matrix products, arithmetic and copies ran while one was open for 4% of the time, Pallas kernels for 0%

profile of v1, /device:TPU:0, one launch (start us, length us, event | category | flops | bytes accessed | tf_op | source)
XLA Modules:
  0.0 119.4 jit_solution(9064427636794711580)
XLA Ops:
  0.6 0.0 copy-start.1
  0.6 0.0 copy-start
  0.7 0.9 constant_dynamic-update-slice_fusion.1
  1.6 0.9 constant_dynamic-update-slice_fusion
  2.5 5.1 %collective-permute-start.2 = (bf16[256,256]{1,0:T(8,128)(2,1)S(1)}, bf16[256,256]{1,0:T(8,128)(2,1)S(1)}, u32[]{:S(2)}, u32[]{:S(2)}) collective-permute-start(bf16[256,256]{1,0:T(8,128)(2,1)S(1)} %constant_dynamic-update-slice_fusion), channel_id=1, source_target_pairs={{0,24},{8,0},{16,8},{24,16},{1,25},{9,1},{17,9},{25,17},{2,26},{10... | collective-permute-start | bytes 393224 | tf_op jit(solution)/shard_map/ppermute | solution.py:160
  7.6 0.0 collective-permute-start.1
  7.6 1.0 collective-permute-start
  8.6 0.7 copy.15
  9.3 0.1 reduce-window.9
  9.4 0.1 reduce
  9.5 1.3 %sub.34.starts_ref = s32[64]{0:T(128)} subtract(s32[64]{0:T(128)S(1)} %reduce, s32[64]{0:T(128)} %param.11) | non-fusion elementwise | flops 64 | bytes 768 | tf_op jit(solution)/shard_map/sub | solution.py:187
  10.8 0.7 broadcast_add_fusion
  11.5 0.1 add_maximum_fusion
  11.5 0.1 max.13
  11.6 0.0 collective-permute-done.2
  11.6 7.2 %collective-permute-done.1 = bf16[256,256]{1,0:T(8,128)(2,1)S(1)} collective-permute-done((bf16[256,256]{1,0:T(8,128)(2,1)S(1)}, bf16[256,256]{1,0:T(8,128)(2,1)S(1)}, u32[]{:S(2)}, u32[]{:S(2)}) %collective-permute-start.1) | collective-permute-done | bytes 131104 | tf_op jit(solution)/shard_map/ppermute | solution.py:160
  18.8 0.0 collective-permute-done
  18.8 0.1 fusion.16
  18.9 2.5 %collective-permute-start.5 = (bf16[4,256,256]{2,1,0:T(8,128)(2,1)S(1)}, bf16[4,256,256]{2,1,0:T(8,128)(2,1)S(1)}, u32[]{:S(2)}, u32[]{:S(2)}) collective-permute-start(bf16[4,256,256]{2,1,0:T(8,128)(2,1)S(1)} %get-tuple-element.16), channel_id=1, source_target_pairs={{0,6},{2,0},{4,2},{6,4},{1,7},{3,1},{5,3},{7,5},{8,14},{10,8},{12,... | collective-permute-start | bytes 1572872 | tf_op jit(solution)/shard_map/ppermute | solution.py:160
  21.4 0.5 collective-permute-start.4
  21.9 0.6 collective-permute-start.3
  22.5 0.2 multiply_bitcast_fusion
  22.7 0.2 copy.21
  22.9 0.3 bitcast_reduce_fusion
  23.2 0.7 copy.16
  23.9 0.5 multiply_add_fusion
  24.4 9.3 %collective-permute-done.5 = bf16[4,256,256]{2,1,0:T(8,128)(2,1)S(1)} collective-permute-done((bf16[4,256,256]{2,1,0:T(8,128)(2,1)S(1)}, bf16[4,256,256]{2,1,0:T(8,128)(2,1)S(1)}, u32[]{:S(2)}, u32[]{:S(2)}) %collective-permute-start.5) | collective-permute-done | bytes 524320 | tf_op jit(solution)/shard_map/ppermute | solution.py:160
  33.7 11.8 %collective-permute-done.4 = bf16[4,256,256]{2,1,0:T(8,128)(2,1)S(1)} collective-permute-done((bf16[4,256,256]{2,1,0:T(8,128)(2,1)S(1)}, bf16[4,256,256]{2,1,0:T(8,128)(2,1)S(1)}, u32[]{:S(2)}, u32[]{:S(2)}) %collective-permute-start.4) | collective-permute-done | bytes 524320 | tf_op jit(solution)/shard_map/ppermute | solution.py:160
  45.6 0.0 collective-permute-done.3
  45.6 2.6 %pad_maximum_fusion = bf16[4,4,256,256]{3,2,1,0:T(8,128)(2,1)} fusion(bf16[1,4,256,256]{3,2,1,0:T(8,128)(2,1)S(1)} %bitcast.63, bf16[1,4,256,256]{3,2,1,0:T(8,128)(2,1)S(1)} %bitcast.64, bf16[1,4,256,256]{3,2,1,0:T(8,128)(2,1)} %bitcast.8, bf16[1,4,256,256]{3,2,1,0:T(8,128)(2,1)S(1)} %get-tuple-element.15), kind=kLoop, calls=%fused_computation | loop fusion | flops 3145728 | bytes 4194304 | tf_op jit(solution)/shard_map/stack | solution.py:164
  48.2 13.3 %shard_map.85 = (bf16[256,1024]{1,0:T(8,128)(2,1)}, f32[32,128,256]{2,1,0:T(8,128)}) custom-call(s32[2]{0:T(128)} %get-tuple-element.8.blk_ref, s32[64]{0:T(128)} %sub.34.starts_ref, s32[34]{0:T(128)} %get-tuple-element.20.srow_ref, s32[34]{0:T(128)} %get-tuple-element.19.dst_ref, bf16[256,1024]{1,0:T(8,128)(2,1)} %q_ref.1, bf16[256,1024]{1,0:T(8,128)(2,1)} %do_ref.1, ...), custom_call_target="tpu_custom_call" | custom-call | flops 6845104128 | bytes 8388608 | tf_op jit(solution)/shard_map/pallas_call | solution.py:240
  61.5 2.1 %fusion.3 = (bf16[4,2,128,256]{3,2,1,0:T(8,128)(2,1)S(1)}, bf16[4,2,128,256]{3,2,1,0:T(8,128)(2,1)S(1)}, bf16[4,2,128,256]{3,2,1,0:T(8,128)(2,1)S(1)}) fusion(f32[4,4,2,128,256]{4,3,2,1,0:T(8,128)} %bitcast.59, s32[]{:T(128)S(6)} %select_n.82, s32[]{:T(128)S(6)} %select_n.86, s32[]{:T(128)S(6)} %select_n.84), kind=kLoop, calls=%fused_computation.10 | loop fusion | bytes 3145740 | tf_op jit(solution)/shard_map/convert_element_type | solution.py:172
  63.6 0.6 collective-permute-start.8
  64.1 1.4 %collective-permute-start.7 = (bf16[4,2,128,256]{3,2,1,0:T(8,128)(2,1)S(1)}, bf16[4,2,128,256]{3,2,1,0:T(8,128)(2,1)S(1)}, u32[]{:S(2)}, u32[]{:S(2)}) collective-permute-start(bf16[4,2,128,256]{3,2,1,0:T(8,128)(2,1)S(1)} %get-tuple-element.11), channel_id=1, source_target_pairs={{0,4},{2,6},{4,0},{6,2},{1,5},{3,7},{5,1},{7,3},{8,12},{10,14},{12... | collective-permute-start | bytes 1572872 | tf_op jit(solution)/shard_map/ppermute | solution.py:160
  65.5 0.2 collective-permute-start.6
  65.7 12.8 %collective-permute-done.8 = bf16[4,2,128,256]{3,2,1,0:T(8,128)(2,1)S(1)} collective-permute-done((bf16[4,2,128,256]{3,2,1,0:T(8,128)(2,1)S(1)}, bf16[4,2,128,256]{3,2,1,0:T(8,128)(2,1)S(1)}, u32[]{:S(2)}, u32[]{:S(2)}) %collective-permute-start.8) | collective-permute-done | bytes 524320 | tf_op jit(solution)/shard_map/ppermute | solution.py:160
  78.4 10.0 %collective-permute-done.7 = bf16[4,2,128,256]{3,2,1,0:T(8,128)(2,1)S(1)} collective-permute-done((bf16[4,2,128,256]{3,2,1,0:T(8,128)(2,1)S(1)}, bf16[4,2,128,256]{3,2,1,0:T(8,128)(2,1)S(1)}, u32[]{:S(2)}, u32[]{:S(2)}) %collective-permute-start.7) | collective-permute-done | bytes 524320 | tf_op jit(solution)/shard_map/ppermute | solution.py:160
  88.4 0.0 collective-permute-done.6
  88.4 1.4 %fusion.1 = f32[4,2,128,256]{3,2,1,0:T(8,128)S(1)} fusion(bf16[4,2,128,256]{3,2,1,0:T(8,128)(2,1)S(1)} %collective-permute-done.8, bf16[4,2,128,256]{3,2,1,0:T(8,128)(2,1)S(1)} %collective-permute-done.7, bf16[4,2,128,256]{3,2,1,0:T(8,128)(2,1)S(1)} %collective-permute-done.6, f32[4,4,2,128,256]{4,3,2,1,0:T(8,128)} %bitcast.60, s32[]{:T(128)S(6)} %select_n.80), kind=kLoop, calls=%fused_computation.6 | loop fusion | flops 1572864 | bytes 3670020 | tf_op jit(solution)/shard_map/add | solution.py:172
  89.8 0.1 fusion.8
  89.9 21.1 %collective-permute-start.11 = (bf16[2,128,256]{2,1,0:T(8,128)(2,1)S(1)}, bf16[2,128,256]{2,1,0:T(8,128)(2,1)S(1)}, u32[]{:S(2)}, u32[]{:S(2)}) collective-permute-start(bf16[2,128,256]{2,1,0:T(8,128)(2,1)S(1)} %get-tuple-element.13), channel_id=1, source_target_pairs={{0,24},{8,0},{16,8},{24,16},{1,25},{9,1},{17,9},{25,17},{2,26},{10... | collective-permute-start | bytes 393224 | tf_op jit(solution)/shard_map/ppermute | solution.py:160
  111.0 0.0 collective-permute-start.10
  111.0 0.6 collective-permute-start.9
  111.6 1.9 %collective-permute-done.11 = bf16[2,128,256]{2,1,0:T(8,128)(2,1)S(1)} collective-permute-done((bf16[2,128,256]{2,1,0:T(8,128)(2,1)S(1)}, bf16[2,128,256]{2,1,0:T(8,128)(2,1)S(1)}, u32[]{:S(2)}, u32[]{:S(2)}) %collective-permute-start.11) | collective-permute-done | bytes 131104 | tf_op jit(solution)/shard_map/ppermute | solution.py:160
  113.5 5.1 %collective-permute-done.10 = bf16[2,128,256]{2,1,0:T(8,128)(2,1)S(1)} collective-permute-done((bf16[2,128,256]{2,1,0:T(8,128)(2,1)S(1)}, bf16[2,128,256]{2,1,0:T(8,128)(2,1)S(1)}, u32[]{:S(2)}, u32[]{:S(2)}) %collective-permute-start.10) | collective-permute-done | bytes 131104 | tf_op jit(solution)/shard_map/ppermute | solution.py:160
  118.6 0.0 collective-permute-done.9
  118.6 0.1 fusion.7
  118.7 0.7 fusion.17
  (2 shorter events, 0.0 us)
Async XLA Ops:
  0.6 21.9 %copy-start.1 = (bf16[256,1024]{1,0:T(8,128)(2,1)S(1)}, bf16[256,1024]{1,0:T(8,128)(2,1)}, u32[]{:S(2)}) copy-start(bf16[256,1024]{1,0:T(8,128)(2,1)} %do_ref.1) | copy-start | bytes 1572868
  0.6 21.9 %copy-start = (bf16[256,1024]{1,0:T(8,128)(2,1)S(1)}, bf16[256,1024]{1,0:T(8,128)(2,1)}, u32[]{:S(2)}) copy-start(bf16[256,1024]{1,0:T(8,128)(2,1)} %param.9) | copy-start | bytes 1572868
  2.5 9.2 %collective-permute-start.2 = (bf16[256,256]{1,0:T(8,128)(2,1)S(1)}, bf16[256,256]{1,0:T(8,128)(2,1)S(1)}, u32[]{:S(2)}, u32[]{:S(2)}) collective-permute-start(bf16[256,256]{1,0:T(8,128)(2,1)S(1)} %constant_dynamic-update-slice_fusion), channel_id=1, source_target_pairs={{0,24},{8,0},{16,8},{24,16},{1,25},{9,1},{17,9},{25,17},{2,26},{10... | collective-permute-start | bytes 393224 | tf_op jit(solution)/shard_map/ppermute | solution.py:160
  7.6 11.2 %collective-permute-start.1 = (bf16[256,256]{1,0:T(8,128)(2,1)S(1)}, bf16[256,256]{1,0:T(8,128)(2,1)S(1)}, u32[]{:S(2)}, u32[]{:S(2)}) collective-permute-start(bf16[256,256]{1,0:T(8,128)(2,1)S(1)} %constant_dynamic-update-slice_fusion), channel_id=1, source_target_pairs={{0,16},{8,24},{16,0},{24,8},{1,17},{9,25},{17,1},{25,9},{2,18},{10... | collective-permute-start | bytes 393224 | tf_op jit(solution)/shard_map/ppermute | solution.py:160
  7.6 11.2 %collective-permute-start = (bf16[256,256]{1,0:T(8,128)(2,1)S(1)}, bf16[256,256]{1,0:T(8,128)(2,1)S(1)}, u32[]{:S(2)}, u32[]{:S(2)}) collective-permute-start(bf16[256,256]{1,0:T(8,128)(2,1)S(1)} %constant_dynamic-update-slice_fusion), channel_id=1, source_target_pairs={{0,8},{8,16},{16,24},{24,0},{1,9},{9,17},{17,25},{25,1},{2,10},{10... | collective-permute-start | bytes 393224 | tf_op jit(solution)/shard_map/ppermute | solution.py:160
  18.9 14.8 %collective-permute-start.5 = (bf16[4,256,256]{2,1,0:T(8,128)(2,1)S(1)}, bf16[4,256,256]{2,1,0:T(8,128)(2,1)S(1)}, u32[]{:S(2)}, u32[]{:S(2)}) collective-permute-start(bf16[4,256,256]{2,1,0:T(8,128)(2,1)S(1)} %get-tuple-element.16), channel_id=1, source_target_pairs={{0,6},{2,0},{4,2},{6,4},{1,7},{3,1},{5,3},{7,5},{8,14},{10,8},{12,... | collective-permute-start | bytes 1572872 | tf_op jit(solution)/shard_map/ppermute | solution.py:160
  21.4 24.2 %collective-permute-start.4 = (bf16[4,256,256]{2,1,0:T(8,128)(2,1)S(1)}, bf16[4,256,256]{2,1,0:T(8,128)(2,1)S(1)}, u32[]{:S(2)}, u32[]{:S(2)}) collective-permute-start(bf16[4,256,256]{2,1,0:T(8,128)(2,1)S(1)} %get-tuple-element.16), channel_id=1, source_target_pairs={{0,4},{2,6},{4,0},{6,2},{1,5},{3,7},{5,1},{7,3},{8,12},{10,14},{12... | collective-permute-start | bytes 1572872 | tf_op jit(solution)/shard_map/ppermute | solution.py:160
  21.9 23.7 %collective-permute-start.3 = (bf16[4,256,256]{2,1,0:T(8,128)(2,1)S(1)}, bf16[4,256,256]{2,1,0:T(8,128)(2,1)}, u32[]{:S(2)}, u32[]{:S(2)}) collective-permute-start(bf16[4,256,256]{2,1,0:T(8,128)(2,1)S(1)} %get-tuple-element.16), channel_id=1, source_target_pairs={{0,2},{2,4},{4,6},{6,0},{1,3},{3,5},{5,7},{7,1},{8,10},{10,12},{12... | collective-permute-start | bytes 1572872 | tf_op jit(solution)/shard_map/ppermute | solution.py:160
  63.6 14.8 %collective-permute-start.8 = (bf16[4,2,128,256]{3,2,1,0:T(8,128)(2,1)S(1)}, bf16[4,2,128,256]{3,2,1,0:T(8,128)(2,1)S(1)}, u32[]{:S(2)}, u32[]{:S(2)}) collective-permute-start(bf16[4,2,128,256]{3,2,1,0:T(8,128)(2,1)S(1)} %get-tuple-element.10), channel_id=1, source_target_pairs={{0,6},{2,0},{4,2},{6,4},{1,7},{3,1},{5,3},{7,5},{8,14},{10,8},{12,... | collective-permute-start | bytes 1572872 | tf_op jit(solution)/shard_map/ppermute | solution.py:160
  64.1 24.3 %collective-permute-start.7 = (bf16[4,2,128,256]{3,2,1,0:T(8,128)(2,1)S(1)}, bf16[4,2,128,256]{3,2,1,0:T(8,128)(2,1)S(1)}, u32[]{:S(2)}, u32[]{:S(2)}) collective-permute-start(bf16[4,2,128,256]{3,2,1,0:T(8,128)(2,1)S(1)} %get-tuple-element.11), channel_id=1, source_target_pairs={{0,4},{2,6},{4,0},{6,2},{1,5},{3,7},{5,1},{7,3},{8,12},{10,14},{12... | collective-permute-start | bytes 1572872 | tf_op jit(solution)/shard_map/ppermute | solution.py:160
  65.5 22.9 %collective-permute-start.6 = (bf16[4,2,128,256]{3,2,1,0:T(8,128)(2,1)S(1)}, bf16[4,2,128,256]{3,2,1,0:T(8,128)(2,1)S(1)}, u32[]{:S(2)}, u32[]{:S(2)}) collective-permute-start(bf16[4,2,128,256]{3,2,1,0:T(8,128)(2,1)S(1)} %get-tuple-element.9), channel_id=1, source_target_pairs={{0,2},{2,4},{4,6},{6,0},{1,3},{3,5},{5,7},{7,1},{8,10},{10,12},{12... | collective-permute-start | bytes 1572872 | tf_op jit(solution)/shard_map/ppermute | solution.py:160
  89.9 23.6 %collective-permute-start.11 = (bf16[2,128,256]{2,1,0:T(8,128)(2,1)S(1)}, bf16[2,128,256]{2,1,0:T(8,128)(2,1)S(1)}, u32[]{:S(2)}, u32[]{:S(2)}) collective-permute-start(bf16[2,128,256]{2,1,0:T(8,128)(2,1)S(1)} %get-tuple-element.13), channel_id=1, source_target_pairs={{0,24},{8,0},{16,8},{24,16},{1,25},{9,1},{17,9},{25,17},{2,26},{10... | collective-permute-start | bytes 393224 | tf_op jit(solution)/shard_map/ppermute | solution.py:160
  111.0 7.6 %collective-permute-start.10 = (bf16[2,128,256]{2,1,0:T(8,128)(2,1)S(1)}, bf16[2,128,256]{2,1,0:T(8,128)(2,1)S(1)}, u32[]{:S(2)}, u32[]{:S(2)}) collective-permute-start(bf16[2,128,256]{2,1,0:T(8,128)(2,1)S(1)} %get-tuple-element.14), channel_id=1, source_target_pairs={{0,16},{8,24},{16,0},{24,8},{1,17},{9,25},{17,1},{25,9},{2,18},{10... | collective-permute-start | bytes 393224 | tf_op jit(solution)/shard_map/ppermute | solution.py:160
  111.0 7.6 %collective-permute-start.9 = (bf16[2,128,256]{2,1,0:T(8,128)(2,1)S(1)}, bf16[2,128,256]{2,1,0:T(8,128)(2,1)S(1)}, u32[]{:S(2)}, u32[]{:S(2)}) collective-permute-start(bf16[2,128,256]{2,1,0:T(8,128)(2,1)S(1)} %get-tuple-element.12), channel_id=1, source_target_pairs={{0,8},{8,16},{16,24},{24,0},{1,9},{9,17},{17,25},{25,1},{2,10},{10... | collective-permute-start | bytes 393224 | tf_op jit(solution)/shard_map/ppermute | solution.py:160

commit v2 on v0

--- a/solution.py
+++ b/solution.py
@@ -10,23 +10,28 @@
 REACH = 16
 
 
-def _bwd_kernel(blk_ref, starts_ref, srow_ref, dst_ref, q_ref, do_ref, kv_hbm,
-                delta_ref, dq_ref, part_ref, qall, doall, dqt, kvbuf, sems, sbuf, dsbuf,
-                *, rows, heads, width, reach, scaling, docs):
+def _bwd_kernel(blk_ref, starts_ref, srow_ref, src_ref, dst_ref, q_ref, do_ref, *rest,
+                rows, heads, width, reach, scaling, docs, pieces):
+    kv_refs = rest[:pieces]
+    (delta_ref, dq_ref, part_ref, qall, doall, dqt, kvbuf, sems, sbuf, dsbuf) = rest[pieces:]
     s = pl.program_id(0)
     win = reach + 1
 
-    def copy(side, i):
+    def copy(side, i, ref):
         row = pl.multiple_of(srow_ref[side * win + i], rows)
         return pltpu.make_async_copy(
-            kv_hbm.at[pl.ds(row, rows)], kvbuf.at[side, i], sems.at[side, i]
+            ref.at[pl.ds(row, rows)], kvbuf.at[side, i], sems.at[side, i]
         )
 
     @pl.when(s == 0)
     def _():
         for side in range(2):
             for i in range(win):
-                copy(side, i).start()
+                which = src_ref[side * win + i]
+                for t in range(pieces):
+                    @pl.when(which == t)
+                    def _():
+                        copy(side, i, kv_refs[t]).start()
         part_ref[...] = jnp.zeros(part_ref.shape, jnp.float32)
 
     b = blk_ref[s]
@@ -54,7 +59,7 @@
     nt = (((1,), (1,)), ((), ()))
     tn = (((0,), (0,)), ((), ()))
     for i in range(win):
-        copy(s, i).wait()
+        copy(s, i, kv_refs[0]).wait()
 
     def scores(c):
         kc = kvbuf[s, c, :, :width]
@@ -143,7 +148,9 @@
 
     kv_local = jnp.concatenate([shared_keys, shared_values], axis=1)
     kv_col = _group_gather(kv_local, n_out, "zp")
-    kv_recv = _group_gather(kv_col, n_in, "w").reshape(n_in * n_out * 2 * rows, 2 * width)
+    kv_pieces = [kv_col.reshape(n_out * 2 * rows, 2 * width)] + [
+        _shift(kv_col, k, n_in, "w").reshape(n_out * 2 * rows, 2 * width) for k in range(1, n_in)
+    ]
 
     me_z = lax.axis_index("zp")
     me_w = lax.axis_index("w")
@@ -153,7 +160,8 @@
     slot = (seq_blk >= n_seq).astype(jnp.int32)
     k_z = (me_z - dev // n_in) % n_out
     k_w = (me_w - dev % n_in) % n_in
-    srow = (((k_w * n_out + k_z) * 2 + slot) * rows).astype(jnp.int32)
+    srow = ((k_z * 2 + slot) * rows).astype(jnp.int32)
+    src_piece = k_w.astype(jnp.int32)
     dst = (dev * 2 + slot).astype(jnp.int32)
 
     prod = out_grad.astype(jnp.float32) * outputs.astype(jnp.float32)
@@ -162,17 +170,17 @@
 
     kernel = functools.partial(
         _bwd_kernel, rows=rows, heads=heads, width=width, reach=REACH, scaling=scaling,
-        docs=doc_lengths.shape[0],
+        docs=doc_lengths.shape[0], pieces=n_in,
     )
     cols = heads * rows
     vec = pl.BlockSpec((None, 1, cols), lambda s, *_: (s, 0, 0))
     grid_spec = pltpu.PrefetchScalarGridSpec(
-        num_scalar_prefetch=4,
+        num_scalar_prefetch=5,
         grid=(2,),
         in_specs=[
             pl.BlockSpec((rows, cols), lambda s, *_: (s, 0)),
             pl.BlockSpec((rows, cols), lambda s, *_: (s, 0)),
-            pl.BlockSpec(memory_space=pl.ANY),
+        ] + [pl.BlockSpec(memory_space=pl.ANY)] * n_in + [
             vec,
         ],
         out_specs=[
@@ -201,7 +209,8 @@
         cost_estimate=pl.CostEstimate(
             flops=flops, transcendentals=2 * 2 * win * rows * cols, bytes_accessed=8 << 20
         ),
-    )(blocks, doc_starts.astype(jnp.int32), srow, dst, queries, out_grad, kv_recv, delta_t)
+    )(blocks, doc_starts.astype(jnp.int32), srow, src_piece, dst, queries, out_grad,
+      *kv_pieces, delta_t)
 
     storage = partial
     storage = storage.reshape(n_out, n_in, 2, rows, 2 * width)

time: 112 us -> 112 us (level)
  starting transfers between devices: 26 us -> 28.3 us
  Pallas kernels: 13.4 us -> 11.8 us
    another operation x2 -> x1, other arithmetic: 2.71 us -> 0.07 us  [_group_gather(): return jnp.stack([x] + [_shift(x, k, n, axis) for k in range(1, n)])]
    ppermute x12, starting transfers between devices: 26 us -> 28.3 us  [_shift(): return lax.ppermute(x, axis, [(i, (i + k) % n) for i in range(n)])]
    pallas_call x1, Pallas kernels: 13.4 us -> 11.8 us  [body(): pl.pallas_call(kernel, grid_spec=grid_spec, out_shape=[jax.ShapeDtypeStru...]
    unnamed x1, other arithmetic: 0.17 us -> 1.37 us
  transfers between devices with their start and end apart: 12 -> 12, of which waited for: 7 -> 9; matrix products, arithmetic and copies ran while one was open for 4% -> 6% of each run, Pallas kernels for 0% -> 0%
where the time goes in v2:
time: 112 us
  waiting for transfers between devices  57.5 us (51%)
  starting transfers between devices  28.3 us (25%)
  Pallas kernels  11.8 us (11%)
  local copies, waits for them, and re-layouts  7.11 us (6%)
  other arithmetic  6.52 us (6%)
    ppermute x12, waiting for transfers between devices, _shift(): return lax.ppermute(x, axis, [(i, (i + k) % n) for i in range(n)])  57.5 us
    ppermute x12, starting transfers between devices, _shift(): return lax.ppermute(x, axis, [(i, (i + k) % n) for i in range(n)])  28.3 us
    pallas_call x1, Pallas kernels, body(): pl.pallas_call(kernel, grid_spec=grid_spec, out_shape=[jax.ShapeDtypeStru...  11.8 us
  transfers between devices with their start and end apart: 12, of which 9 were waited for; matrix products, arithmetic and copies ran while one was open for 6% of the time, Pallas kernels for 0%

profile of v2, /device:TPU:0, one launch (start us, length us, event | category | flops | bytes accessed | tf_op | source)
XLA Modules:
  0.0 111.9 jit_solution(12219581894769157467)
XLA Ops:
  0.6 0.9 constant_dynamic-update-slice_fusion.1
  1.5 0.9 constant_dynamic-update-slice_fusion
  2.3 5.1 %collective-permute-start.2 = (bf16[256,256]{1,0:T(8,128)(2,1)S(1)}, bf16[256,256]{1,0:T(8,128)(2,1)S(1)}, u32[]{:S(2)}, u32[]{:S(2)}) collective-permute-start(bf16[256,256]{1,0:T(8,128)(2,1)S(1)} %constant_dynamic-update-slice_fusion), channel_id=1, source_target_pairs={{0,24},{8,0},{16,8},{24,16},{1,25},{9,1},{17,9},{25,17},{2,26},{10... | collective-permute-start | bytes 393224 | tf_op jit(solution)/shard_map/ppermute | solution.py:119
  7.5 0.0 collective-permute-start.1
  7.5 1.0 collective-permute-start
  8.5 0.7 copy.15
  9.2 0.1 reduce-window.9
  9.3 0.1 reduce
  9.4 1.2 %sub.34.starts_ref = s32[64]{0:T(128)} subtract(s32[64]{0:T(128)S(1)} %reduce, s32[64]{0:T(128)} %param.11) | non-fusion elementwise | flops 64 | bytes 768 | tf_op jit(solution)/shard_map/sub | solution.py:146
  10.6 0.7 broadcast_add_fusion
  11.3 1.4 %multiply_bitcast_fusion = f32[32,8,8,128]{3,1,2,0:T(8,128)S(1)} fusion(bf16[256,1024]{1,0:T(8,128)(2,1)} %param.9, bf16[256,1024]{1,0:T(8,128)(2,1)} %do_ref.1), kind=kLoop, calls=%fused_computation.7 | loop fusion | flops 786432 | bytes 2097152
  12.7 0.1 add_maximum_fusion
  12.7 0.1 max.13
  12.8 0.2 copy.21
  13.0 0.0 collective-permute-done.2
  13.0 5.7 %collective-permute-done.1 = bf16[256,256]{1,0:T(8,128)(2,1)S(1)} collective-permute-done((bf16[256,256]{1,0:T(8,128)(2,1)S(1)}, bf16[256,256]{1,0:T(8,128)(2,1)S(1)}, u32[]{:S(2)}, u32[]{:S(2)}) %collective-permute-start.1) | collective-permute-done | bytes 131104 | tf_op jit(solution)/shard_map/ppermute | solution.py:119
  18.7 0.0 collective-permute-done
  18.7 0.1 pad_maximum_fusion
  18.8 1.5 %collective-permute-start.3 = (bf16[4,256,256]{2,1,0:T(8,128)(2,1)S(1)}, bf16[4,256,256]{2,1,0:T(8,128)(2,1)S(1)}, u32[]{:S(2)}, u32[]{:S(2)}) collective-permute-start(bf16[4,256,256]{2,1,0:T(8,128)(2,1)S(1)} %pad_maximum_fusion), channel_id=1, source_target_pairs={{0,2},{2,4},{4,6},{6,0},{1,3},{3,5},{5,7},{7,1},{8,10},{10,12},{12... | collective-permute-start | bytes 1572872 | tf_op jit(solution)/shard_map/ppermute | solution.py:119
  20.3 1.5 %collective-permute-start.4 = (bf16[4,256,256]{2,1,0:T(8,128)(2,1)S(1)}, bf16[4,256,256]{2,1,0:T(8,128)(2,1)S(1)}, u32[]{:S(2)}, u32[]{:S(2)}) collective-permute-start(bf16[4,256,256]{2,1,0:T(8,128)(2,1)S(1)} %pad_maximum_fusion), channel_id=1, source_target_pairs={{0,4},{2,6},{4,0},{6,2},{1,5},{3,7},{5,1},{7,3},{8,12},{10,14},{12... | collective-permute-start | bytes 1572872 | tf_op jit(solution)/shard_map/ppermute | solution.py:119
  21.8 1.4 %collective-permute-start.5 = (bf16[4,256,256]{2,1,0:T(8,128)(2,1)S(1)}, bf16[4,256,256]{2,1,0:T(8,128)(2,1)S(1)}, u32[]{:S(2)}, u32[]{:S(2)}) collective-permute-start(bf16[4,256,256]{2,1,0:T(8,128)(2,1)S(1)} %pad_maximum_fusion), channel_id=1, source_target_pairs={{0,6},{2,0},{4,2},{6,4},{1,7},{3,1},{5,3},{7,5},{8,14},{10,8},{12,... | collective-permute-start | bytes 1572872 | tf_op jit(solution)/shard_map/ppermute | solution.py:119
  23.3 0.3 bitcast_reduce_fusion
  23.6 0.7 copy.16
  24.3 0.5 and_select_fusion
  24.8 0.6 fusion.16.srow_ref
  25.4 9.1 %collective-permute-done.3 = bf16[4,256,256]{2,1,0:T(8,128)(2,1)S(1)} collective-permute-done((bf16[4,256,256]{2,1,0:T(8,128)(2,1)S(1)}, bf16[4,256,256]{2,1,0:T(8,128)(2,1)S(1)}, u32[]{:S(2)}, u32[]{:S(2)}) %collective-permute-start.3) | collective-permute-done | bytes 524320 | tf_op jit(solution)/shard_map/ppermute | solution.py:119
  34.6 9.6 %collective-permute-done.4 = bf16[4,256,256]{2,1,0:T(8,128)(2,1)S(1)} collective-permute-done((bf16[4,256,256]{2,1,0:T(8,128)(2,1)S(1)}, bf16[4,256,256]{2,1,0:T(8,128)(2,1)S(1)}, u32[]{:S(2)}, u32[]{:S(2)}) %collective-permute-start.4) | collective-permute-done | bytes 524320 | tf_op jit(solution)/shard_map/ppermute | solution.py:119
  44.2 0.1 collective-permute-done.5
  44.3 0.7 copy-done.2
  45.0 0.2 copy-done.3
  45.2 11.8 %shard_map.85 = (bf16[256,1024]{1,0:T(8,128)(2,1)}, f32[32,128,256]{2,1,0:T(8,128)}) custom-call(s32[2]{0:T(128)} %get-tuple-element.10.blk_ref, s32[64]{0:T(128)} %sub.34.starts_ref, s32[34]{0:T(128)} %fusion.16.srow_ref, s32[34]{0:T(128)} %get-tuple-element.7.src_ref, s32[34]{0:T(128)} %get-tuple-element.19.dst_ref, bf16[256,1024]{1,0:T(8,128)(2,1)} %q_ref.1, ...), custom_call_target="tpu_custom_call" | custom-call | flops 6845104128 | bytes 8388608 | tf_op jit(solution)/shard_map/pallas_call | solution.py:201
  57.0 2.1 %fusion.3 = (bf16[4,2,128,256]{3,2,1,0:T(8,128)(2,1)S(1)}, bf16[4,2,128,256]{3,2,1,0:T(8,128)(2,1)S(1)}, bf16[4,2,128,256]{3,2,1,0:T(8,128)(2,1)S(1)}) fusion(f32[4,4,2,128,256]{4,3,2,1,0:T(8,128)} %bitcast.56, s32[]{:T(128)S(6)} %select_n.82, s32[]{:T(128)S(6)} %select_n.86, s32[]{:T(128)S(6)} %select_n.84), kind=kLoop, calls=%fused_computation.9 | loop fusion | bytes 3145740 | tf_op jit(solution)/shard_map/convert_element_type | solution.py:131
  59.1 1.6 %collective-permute-start.8 = (bf16[4,2,128,256]{3,2,1,0:T(8,128)(2,1)S(1)}, bf16[4,2,128,256]{3,2,1,0:T(8,128)(2,1)S(1)}, u32[]{:S(2)}, u32[]{:S(2)}) collective-permute-start(bf16[4,2,128,256]{3,2,1,0:T(8,128)(2,1)S(1)} %get-tuple-element.12), channel_id=1, source_target_pairs={{0,6},{2,0},{4,2},{6,4},{1,7},{3,1},{5,3},{7,5},{8,14},{10,8},{12,... | collective-permute-start | bytes 1572872 | tf_op jit(solution)/shard_map/ppermute | solution.py:119
  60.7 1.6 %collective-permute-start.7 = (bf16[4,2,128,256]{3,2,1,0:T(8,128)(2,1)S(1)}, bf16[4,2,128,256]{3,2,1,0:T(8,128)(2,1)S(1)}, u32[]{:S(2)}, u32[]{:S(2)}) collective-permute-start(bf16[4,2,128,256]{3,2,1,0:T(8,128)(2,1)S(1)} %get-tuple-element.13), channel_id=1, source_target_pairs={{0,4},{2,6},{4,0},{6,2},{1,5},{3,7},{5,1},{7,3},{8,12},{10,14},{12... | collective-permute-start | bytes 1572872 | tf_op jit(solution)/shard_map/ppermute | solution.py:119
  62.4 0.0 collective-permute-start.6
  62.4 11.6 %collective-permute-done.8 = bf16[4,2,128,256]{3,2,1,0:T(8,128)(2,1)S(1)} collective-permute-done((bf16[4,2,128,256]{3,2,1,0:T(8,128)(2,1)S(1)}, bf16[4,2,128,256]{3,2,1,0:T(8,128)(2,1)S(1)}, u32[]{:S(2)}, u32[]{:S(2)}) %collective-permute-start.8) | collective-permute-done | bytes 524320 | tf_op jit(solution)/shard_map/ppermute | solution.py:119
  74.0 0.1 collective-permute-done.7
  74.1 10.3 %collective-permute-done.6 = bf16[4,2,128,256]{3,2,1,0:T(8,128)(2,1)S(1)} collective-permute-done((bf16[4,2,128,256]{3,2,1,0:T(8,128)(2,1)S(1)}, bf16[4,2,128,256]{3,2,1,0:T(8,128)(2,1)S(1)}, u32[]{:S(2)}, u32[]{:S(2)}) %collective-permute-start.6) | collective-permute-done | bytes 524320 | tf_op jit(solution)/shard_map/ppermute | solution.py:119
  84.3 1.4 %fusion.1 = f32[4,2,128,256]{3,2,1,0:T(8,128)S(1)} fusion(bf16[4,2,128,256]{3,2,1,0:T(8,128)(2,1)S(1)} %collective-permute-done.8, bf16[4,2,128,256]{3,2,1,0:T(8,128)(2,1)S(1)} %collective-permute-done.7, bf16[4,2,128,256]{3,2,1,0:T(8,128)(2,1)S(1)} %collective-permute-done.6, f32[4,4,2,128,256]{4,3,2,1,0:T(8,128)} %bitcast.57, s32[]{:T(128)S(6)} %select_n.80), kind=kLoop, calls=%fused_computation.5 | loop fusion | flops 1572864 | bytes 3670020 | tf_op jit(solution)/shard_map/add | solution.py:131
  85.8 0.1 fusion.8
  85.8 9.2 %collective-permute-start.11 = (bf16[2,128,256]{2,1,0:T(8,128)(2,1)S(1)}, bf16[2,128,256]{2,1,0:T(8,128)(2,1)S(1)}, u32[]{:S(2)}, u32[]{:S(2)}) collective-permute-start(bf16[2,128,256]{2,1,0:T(8,128)(2,1)S(1)} %get-tuple-element.15), channel_id=1, source_target_pairs={{0,24},{8,0},{16,8},{24,16},{1,25},{9,1},{17,9},{25,17},{2,26},{10... | collective-permute-start | bytes 393224 | tf_op jit(solution)/shard_map/ppermute | solution.py:119
  95.0 5.2 %collective-permute-start.10 = (bf16[2,128,256]{2,1,0:T(8,128)(2,1)S(1)}, bf16[2,128,256]{2,1,0:T(8,128)(2,1)S(1)}, u32[]{:S(2)}, u32[]{:S(2)}) collective-permute-start(bf16[2,128,256]{2,1,0:T(8,128)(2,1)S(1)} %get-tuple-element.16), channel_id=1, source_target_pairs={{0,16},{8,24},{16,0},{24,8},{1,17},{9,25},{17,1},{25,9},{2,18},{10... | collective-permute-start | bytes 393224 | tf_op jit(solution)/shard_map/ppermute | solution.py:119
  100.2 0.0 collective-permute-start.9
  100.3 1.5 %collective-permute-done.11 = bf16[2,128,256]{2,1,0:T(8,128)(2,1)S(1)} collective-permute-done((bf16[2,128,256]{2,1,0:T(8,128)(2,1)S(1)}, bf16[2,128,256]{2,1,0:T(8,128)(2,1)S(1)}, u32[]{:S(2)}, u32[]{:S(2)}) %collective-permute-start.11) | collective-permute-done | bytes 131104 | tf_op jit(solution)/shard_map/ppermute | solution.py:119
  101.7 9.5 %collective-permute-done.10 = bf16[2,128,256]{2,1,0:T(8,128)(2,1)S(1)} collective-permute-done((bf16[2,128,256]{2,1,0:T(8,128)(2,1)S(1)}, bf16[2,128,256]{2,1,0:T(8,128)(2,1)S(1)}, u32[]{:S(2)}, u32[]{:S(2)}) %collective-permute-start.10) | collective-permute-done | bytes 131104 | tf_op jit(solution)/shard_map/ppermute | solution.py:119
  111.2 0.0 collective-permute-done.9
  111.2 0.1 fusion.7
  111.3 0.7 fusion.17
  (6 shorter events, 0.0 us)
Async XLA Ops:
  2.3 10.7 %collective-permute-start.2 = (bf16[256,256]{1,0:T(8,128)(2,1)S(1)}, bf16[256,256]{1,0:T(8,128)(2,1)S(1)}, u32[]{:S(2)}, u32[]{:S(2)}) collective-permute-start(bf16[256,256]{1,0:T(8,128)(2,1)S(1)} %constant_dynamic-update-slice_fusion), channel_id=1, source_target_pairs={{0,24},{8,0},{16,8},{24,16},{1,25},{9,1},{17,9},{25,17},{2,26},{10... | collective-permute-start | bytes 393224 | tf_op jit(solution)/shard_map/ppermute | solution.py:119
  7.5 11.2 %collective-permute-start.1 = (bf16[256,256]{1,0:T(8,128)(2,1)S(1)}, bf16[256,256]{1,0:T(8,128)(2,1)S(1)}, u32[]{:S(2)}, u32[]{:S(2)}) collective-permute-start(bf16[256,256]{1,0:T(8,128)(2,1)S(1)} %constant_dynamic-update-slice_fusion), channel_id=1, source_target_pairs={{0,16},{8,24},{16,0},{24,8},{1,17},{9,25},{17,1},{25,9},{2,18},{10... | collective-permute-start | bytes 393224 | tf_op jit(solution)/shard_map/ppermute | solution.py:119
  7.5 11.2 %collective-permute-start = (bf16[256,256]{1,0:T(8,128)(2,1)S(1)}, bf16[256,256]{1,0:T(8,128)(2,1)S(1)}, u32[]{:S(2)}, u32[]{:S(2)}) collective-permute-start(bf16[256,256]{1,0:T(8,128)(2,1)S(1)} %constant_dynamic-update-slice_fusion), channel_id=1, source_target_pairs={{0,8},{8,16},{16,24},{24,0},{1,9},{9,17},{17,25},{25,1},{2,10},{10... | collective-permute-start | bytes 393224 | tf_op jit(solution)/shard_map/ppermute | solution.py:119
  18.8 25.5 %copy-start = (bf16[4,256,256]{2,1,0:T(8,128)(2,1)}, bf16[4,256,256]{2,1,0:T(8,128)(2,1)S(1)}, u32[]{:S(2)}) copy-start(bf16[4,256,256]{2,1,0:T(8,128)(2,1)S(1)} %pad_maximum_fusion) | copy-start | bytes 1572868
  18.8 15.8 %collective-permute-start.3 = (bf16[4,256,256]{2,1,0:T(8,128)(2,1)S(1)}, bf16[4,256,256]{2,1,0:T(8,128)(2,1)S(1)}, u32[]{:S(2)}, u32[]{:S(2)}) collective-permute-start(bf16[4,256,256]{2,1,0:T(8,128)(2,1)S(1)} %pad_maximum_fusion), channel_id=1, source_target_pairs={{0,2},{2,4},{4,6},{6,0},{1,3},{3,5},{5,7},{7,1},{8,10},{10,12},{12... | collective-permute-start | bytes 1572872 | tf_op jit(solution)/shard_map/ppermute | solution.py:119
  20.3 23.9 %collective-permute-start.4 = (bf16[4,256,256]{2,1,0:T(8,128)(2,1)S(1)}, bf16[4,256,256]{2,1,0:T(8,128)(2,1)S(1)}, u32[]{:S(2)}, u32[]{:S(2)}) collective-permute-start(bf16[4,256,256]{2,1,0:T(8,128)(2,1)S(1)} %pad_maximum_fusion), channel_id=1, source_target_pairs={{0,4},{2,6},{4,0},{6,2},{1,5},{3,7},{5,1},{7,3},{8,12},{10,14},{12... | collective-permute-start | bytes 1572872 | tf_op jit(solution)/shard_map/ppermute | solution.py:119
  21.8 22.5 %collective-permute-start.5 = (bf16[4,256,256]{2,1,0:T(8,128)(2,1)S(1)}, bf16[4,256,256]{2,1,0:T(8,128)(2,1)S(1)}, u32[]{:S(2)}, u32[]{:S(2)}) collective-permute-start(bf16[4,256,256]{2,1,0:T(8,128)(2,1)S(1)} %pad_maximum_fusion), channel_id=1, source_target_pairs={{0,6},{2,0},{4,2},{6,4},{1,7},{3,1},{5,3},{7,5},{8,14},{10,8},{12,... | collective-permute-start | bytes 1572872 | tf_op jit(solution)/shard_map/ppermute | solution.py:119
  34.6 9.7 %copy-start.1 = (bf16[4,256,256]{2,1,0:T(8,128)(2,1)}, bf16[4,256,256]{2,1,0:T(8,128)(2,1)S(1)}, u32[]{:S(2)}) copy-start(bf16[4,256,256]{2,1,0:T(8,128)(2,1)S(1)} %collective-permute-done.3) | copy-start | bytes 1572868
  44.2 0.8 copy-start.2
  44.3 0.9 copy-start.3
  59.1 14.8 %collective-permute-start.8 = (bf16[4,2,128,256]{3,2,1,0:T(8,128)(2,1)S(1)}, bf16[4,2,128,256]{3,2,1,0:T(8,128)(2,1)S(1)}, u32[]{:S(2)}, u32[]{:S(2)}) collective-permute-start(bf16[4,2,128,256]{3,2,1,0:T(8,128)(2,1)S(1)} %get-tuple-element.12), channel_id=1, source_target_pairs={{0,6},{2,0},{4,2},{6,4},{1,7},{3,1},{5,3},{7,5},{8,14},{10,8},{12,... | collective-permute-start | bytes 1572872 | tf_op jit(solution)/shard_map/ppermute | solution.py:119
  60.7 13.3 %collective-permute-start.7 = (bf16[4,2,128,256]{3,2,1,0:T(8,128)(2,1)S(1)}, bf16[4,2,128,256]{3,2,1,0:T(8,128)(2,1)S(1)}, u32[]{:S(2)}, u32[]{:S(2)}) collective-permute-start(bf16[4,2,128,256]{3,2,1,0:T(8,128)(2,1)S(1)} %get-tuple-element.13), channel_id=1, source_target_pairs={{0,4},{2,6},{4,0},{6,2},{1,5},{3,7},{5,1},{7,3},{8,12},{10,14},{12... | collective-permute-start | bytes 1572872 | tf_op jit(solution)/shard_map/ppermute | solution.py:119
  62.4 21.9 %collective-permute-start.6 = (bf16[4,2,128,256]{3,2,1,0:T(8,128)(2,1)S(1)}, bf16[4,2,128,256]{3,2,1,0:T(8,128)(2,1)S(1)}, u32[]{:S(2)}, u32[]{:S(2)}) collective-permute-start(bf16[4,2,128,256]{3,2,1,0:T(8,128)(2,1)S(1)} %get-tuple-element.11), channel_id=1, source_target_pairs={{0,2},{2,4},{4,6},{6,0},{1,3},{3,5},{5,7},{7,1},{8,10},{10,12},{12... | collective-permute-start | bytes 1572872 | tf_op jit(solution)/shard_map/ppermute | solution.py:119
  85.8 15.9 %collective-permute-start.11 = (bf16[2,128,256]{2,1,0:T(8,128)(2,1)S(1)}, bf16[2,128,256]{2,1,0:T(8,128)(2,1)S(1)}, u32[]{:S(2)}, u32[]{:S(2)}) collective-permute-start(bf16[2,128,256]{2,1,0:T(8,128)(2,1)S(1)} %get-tuple-element.15), channel_id=1, source_target_pairs={{0,24},{8,0},{16,8},{24,16},{1,25},{9,1},{17,9},{25,17},{2,26},{10... | collective-permute-start | bytes 393224 | tf_op jit(solution)/shard_map/ppermute | solution.py:119
  95.0 16.2 %collective-permute-start.10 = (bf16[2,128,256]{2,1,0:T(8,128)(2,1)S(1)}, bf16[2,128,256]{2,1,0:T(8,128)(2,1)S(1)}, u32[]{:S(2)}, u32[]{:S(2)}) collective-permute-start(bf16[2,128,256]{2,1,0:T(8,128)(2,1)S(1)} %get-tuple-element.16), channel_id=1, source_target_pairs={{0,16},{8,24},{16,0},{24,8},{1,17},{9,25},{17,1},{25,9},{2,18},{10... | collective-permute-start | bytes 393224 | tf_op jit(solution)/shard_map/ppermute | solution.py:119
  100.2 11.0 %collective-permute-start.9 = (bf16[2,128,256]{2,1,0:T(8,128)(2,1)S(1)}, bf16[2,128,256]{2,1,0:T(8,128)(2,1)S(1)}, u32[]{:S(2)}, u32[]{:S(2)}) collective-permute-start(bf16[2,128,256]{2,1,0:T(8,128)(2,1)S(1)} %get-tuple-element.14), channel_id=1, source_target_pairs={{0,8},{8,16},{16,24},{24,0},{1,9},{9,17},{17,25},{25,1},{2,10},{10... | collective-permute-start | bytes 393224 | tf_op jit(solution)/shard_map/ppermute | solution.py:119

commit v3 on v2

--- a/solution.py
+++ b/solution.py
@@ -1,6 +1,7 @@
 import functools
 
 import jax
+import numpy as np
 import jax.numpy as jnp
 from jax import lax
 from jax.experimental import pallas as pl
@@ -115,6 +116,35 @@
         dq_ref[:, h * width:(h + 1) * width] = (piece.T * scaling).astype(jnp.bfloat16)
 
 
+def _plane_tables(n_seq, n_out, n_in, reach):
+    def needs(dp, d, slot):
+        j = d if slot == 0 else 2 * n_seq - 1 - d
+        up = 2 * n_seq - 1 - dp
+        return (dp - reach <= j <= dp) or (up - reach <= j <= up)
+
+    lists = {}
+    for sr in range(n_seq):
+        zs, ws = divmod(sr, n_in)
+        for k in range(1, n_in):
+            rr = zs * n_in + (ws + k) % n_in
+            got = []
+            for e in range(2 * n_out):
+                kz, slot = divmod(e, 2)
+                d = ((zs - kz) % n_out) * n_in + ws
+                if needs(rr, d, slot):
+                    got.append(e)
+            lists[sr, k] = got
+    most = max(len(v) for v in lists.values())
+    send = np.zeros((n_seq, n_in - 1, most), np.int32)
+    where = np.zeros((n_seq, n_in - 1, 2 * n_out), np.int32)
+    for (sr, k), got in lists.items():
+        padded = got + [got[0] if got else 0] * (most - len(got))
+        send[sr, k - 1] = padded
+        for i, e in enumerate(got):
+            where[sr, k - 1, e] = i
+    return most, send, where
+
+
 def _shift(x, k, n, axis):
     return lax.ppermute(x, axis, [(i, (i + k) % n) for i in range(n)])
 
@@ -148,9 +178,13 @@
 
     kv_local = jnp.concatenate([shared_keys, shared_values], axis=1)
     kv_col = _group_gather(kv_local, n_out, "zp")
-    kv_pieces = [kv_col.reshape(n_out * 2 * rows, 2 * width)] + [
-        _shift(kv_col, k, n_in, "w").reshape(n_out * 2 * rows, 2 * width) for k in range(1, n_in)
-    ]
+    most, send_np, where_np = _plane_tables(n_seq, n_out, n_in, REACH)
+    send_tab = jnp.asarray(send_np)[rank]
+    entries = kv_col.reshape(n_out * 2, rows, 2 * width)
+    kv_pieces = [kv_col.reshape(n_out * 2 * rows, 2 * width)]
+    for k in range(1, n_in):
+        chosen = jnp.take(entries, send_tab[k - 1], axis=0)
+        kv_pieces.append(_shift(chosen, k, n_in, "w").reshape(most * rows, 2 * width))
 
     me_z = lax.axis_index("zp")
     me_w = lax.axis_index("w")
@@ -160,7 +194,10 @@
     slot = (seq_blk >= n_seq).astype(jnp.int32)
     k_z = (me_z - dev // n_in) % n_out
     k_w = (me_w - dev % n_in) % n_in
-    srow = ((k_z * 2 + slot) * rows).astype(jnp.int32)
+    entry = k_z * 2 + slot
+    sender = me_z * n_in + dev % n_in
+    pos = jnp.asarray(where_np)[sender, jnp.maximum(k_w - 1, 0), entry]
+    srow = (jnp.where(k_w == 0, entry, pos) * rows).astype(jnp.int32)
     src_piece = k_w.astype(jnp.int32)
     dst = (dev * 2 + slot).astype(jnp.int32)
 

time: 112 us -> 110 us (0.982)
  waiting for transfers between devices: 57.5 us -> 48.6 us
  starting transfers between devices: 28.3 us -> 32.9 us
  local copies, waits for them, and re-layouts: 7.11 us -> 10.1 us
    ppermute x12, waiting for transfers between devices: 57.5 us -> 48.6 us  [_shift(): return lax.ppermute(x, axis, [(i, (i + k) % n) for i in range(n)])]
    ppermute x12, starting transfers between devices: 28.3 us -> 32.9 us  [_shift(): return lax.ppermute(x, axis, [(i, (i + k) % n) for i in range(n)])]
    gather x0 -> x4, local copies, waits for them, and re-layouts: none -> 2.91 us  [the longest x3 1.71 us: body(): chosen = jnp.take(entries, send_tab[k - 1], axis=0)]
  transfers between devices with their start and end apart: 12 -> 12, of which waited for: 9 -> 8; matrix products, arithmetic and copies ran while one was open for 6% -> 7% of each run, Pallas kernels for 0% -> 0%
where the time goes in v3:
time: 110 us; the launch traced here: 109 us
  waiting for transfers between devices  48.6 us (44%)
  starting transfers between devices  32.9 us (30%)
  Pallas kernels  11 us (10%)
  local copies, waits for them, and re-layouts  10.1 us (9%)
  other arithmetic  5.67 us (5%)
    ppermute x12, waiting for transfers between devices, _shift(): return lax.ppermute(x, axis, [(i, (i + k) % n) for i in range(n)])  48.6 us
    ppermute x12, starting transfers between devices, _shift(): return lax.ppermute(x, axis, [(i, (i + k) % n) for i in range(n)])  32.9 us
    pallas_call x1, Pallas kernels, body(): pl.pallas_call(kernel, grid_spec=grid_spec, out_shape=[jax.ShapeDtypeStru...  11 us
  transfers between devices with their start and end apart: 12, of which 8 were waited for; matrix products, arithmetic and copies ran while one was open for 7% of the time, Pallas kernels for 0%

profile of v3, /device:TPU:0, one launch (start us, length us, event | category | flops | bytes accessed | tf_op | source)
XLA Modules:
  0.0 109.0 jit_solution(8583387918958978144)
XLA Ops:
  0.6 0.9 constant_dynamic-update-slice_fusion.1
  1.5 0.9 constant_dynamic-update-slice_fusion
  2.4 5.1 %collective-permute-start.2 = (bf16[256,256]{1,0:T(8,128)(2,1)S(1)}, bf16[256,256]{1,0:T(8,128)(2,1)S(1)}, u32[]{:S(2)}, u32[]{:S(2)}) collective-permute-start(bf16[256,256]{1,0:T(8,128)(2,1)S(1)} %constant_dynamic-update-slice_fusion), channel_id=1, source_target_pairs={{0,24},{8,0},{16,8},{24,16},{1,25},{9,1},{17,9},{25,17},{2,26},{10... | collective-permute-start | bytes 393224 | tf_op jit(solution)/shard_map/ppermute | solution.py:149
  7.5 1.0 collective-permute-start
  8.5 0.6 broadcast_add_fusion
  9.1 0.1 add_maximum_fusion
  9.2 0.7 constant_dynamic-slice_fusion
  9.9 1.4 %multiply_bitcast_fusion = f32[32,8,8,128]{3,1,2,0:T(8,128)S(1)} fusion(bf16[256,1024]{1,0:T(8,128)(2,1)} %param.13, bf16[256,1024]{1,0:T(8,128)(2,1)} %do_ref.1), kind=kLoop, calls=%fused_computation.11 | loop fusion | flops 786432 | bytes 2097152
  11.3 0.2 copy.23
  11.5 0.3 bitcast_reduce_fusion
  11.8 0.1 max.36
  11.9 0.1 max.35
  12.0 0.1 copy.17
  12.1 0.1 reduce-window.9
  12.2 0.1 reduce
  12.3 0.5 sub.81.starts_ref
  12.8 0.7 copy.18
  13.5 5.2 %collective-permute-done.1 = bf16[256,256]{1,0:T(8,128)(2,1)S(1)} collective-permute-done((bf16[256,256]{1,0:T(8,128)(2,1)S(1)}, bf16[256,256]{1,0:T(8,128)(2,1)S(1)}, u32[]{:S(2)}, u32[]{:S(2)}) %collective-permute-start.1) | collective-permute-done | bytes 131104 | tf_op jit(solution)/shard_map/ppermute | solution.py:149
  18.7 0.1 pad_maximum_fusion
  18.8 0.6 gather_fusion.1
  19.4 0.1 broadcast_select_fusion.2
  19.5 1.5 %collective-permute-start.3 = (bf16[6,128,256]{2,1,0:T(8,128)(2,1)S(1)}, bf16[6,128,256]{2,1,0:T(8,128)(2,1)S(1)}, u32[]{:S(2)}, u32[]{:S(2)}) collective-permute-start(bf16[6,128,256]{2,1,0:T(8,128)(2,1)S(1)} %broadcast_select_fusion.2), channel_id=1, source_target_pairs={{0,2},{2,4},{4,6},{6,0},{1,3},{3,5},{5,7},{7,1},{8,10},{10,12},{12... | collective-permute-start | bytes 1179656 | tf_op jit(solution)/shard_map/ppermute | solution.py:149
  21.0 0.6 gather_fusion.2
  21.6 0.1 broadcast_select_fusion.1
  21.7 1.6 %collective-permute-start.4 = (bf16[6,128,256]{2,1,0:T(8,128)(2,1)S(1)}, bf16[6,128,256]{2,1,0:T(8,128)(2,1)S(1)}, u32[]{:S(2)}, u32[]{:S(2)}) collective-permute-start(bf16[6,128,256]{2,1,0:T(8,128)(2,1)S(1)} %broadcast_select_fusion.1), channel_id=1, source_target_pairs={{0,4},{2,6},{4,0},{6,2},{1,5},{3,7},{5,1},{7,3},{8,12},{10,14},{12... | collective-permute-start | bytes 1179656 | tf_op jit(solution)/shard_map/ppermute | solution.py:149
  23.3 0.6 gather_fusion.3
  23.9 0.1 broadcast_select_fusion
  24.0 1.5 %collective-permute-start.5 = (bf16[6,128,256]{2,1,0:T(8,128)(2,1)S(1)}, bf16[6,128,256]{2,1,0:T(8,128)(2,1)S(1)}, u32[]{:S(2)}, u32[]{:S(2)}) collective-permute-start(bf16[6,128,256]{2,1,0:T(8,128)(2,1)S(1)} %broadcast_select_fusion), channel_id=1, source_target_pairs={{0,6},{2,0},{4,2},{6,4},{1,7},{3,1},{5,3},{7,5},{8,14},{10,8},{12,... | collective-permute-start | bytes 1179656 | tf_op jit(solution)/shard_map/ppermute | solution.py:149
  25.5 1.2 %gather_fusion = s32[34]{0:T(128)S(1)} fusion(s32[16,3,8]{2,1,0:T(4,128)S(1)} %copy-done, s32[34]{0:T(128)S(1)} %fusion.31), kind=kCustom, calls=%fused_computation.3 | custom fusion | bytes 680 | tf_op jit(solution)/shard_map/gather | solution.py:199
  26.7 0.6 fusion.12
  27.3 5.1 %collective-permute-done.3 = bf16[6,128,256]{2,1,0:T(8,128)(2,1)S(1)} collective-permute-done((bf16[6,128,256]{2,1,0:T(8,128)(2,1)S(1)}, bf16[6,128,256]{2,1,0:T(8,128)(2,1)S(1)}, u32[]{:S(2)}, u32[]{:S(2)}) %collective-permute-start.3) | collective-permute-done | bytes 393248 | tf_op jit(solution)/shard_map/ppermute | solution.py:149
  32.5 6.8 %collective-permute-done.4 = bf16[6,128,256]{2,1,0:T(8,128)(2,1)S(1)} collective-permute-done((bf16[6,128,256]{2,1,0:T(8,128)(2,1)S(1)}, bf16[6,128,256]{2,1,0:T(8,128)(2,1)S(1)}, u32[]{:S(2)}, u32[]{:S(2)}) %collective-permute-start.4) | collective-permute-done | bytes 393248 | tf_op jit(solution)/shard_map/ppermute | solution.py:149
  39.3 0.1 collective-permute-done.5
  39.4 0.7 copy-done.4
  40.1 0.2 copy-done.5
  40.2 11.0 %shard_map.103 = (bf16[256,1024]{1,0:T(8,128)(2,1)}, f32[32,128,256]{2,1,0:T(8,128)}) custom-call(s32[2]{0:T(128)} %get-tuple-element.17.blk_ref, s32[64]{0:T(128)} %sub.81.starts_ref, s32[34]{0:T(128)} %get-tuple-element.14.srow_ref, s32[34]{0:T(128)} %get-tuple-element.15.src_ref, s32[34]{0:T(128)} %get-tuple-element.30.dst_ref, bf16[256,1024]{1,0:T(8,128)(2,1)} %q_ref.1, ...), custom_call_target="tpu_custom_call" | custom-call | flops 6845104128 | bytes 8388608 | tf_op jit(solution)/shard_map/pallas_call | solution.py:238
  51.2 2.1 %fusion.3 = (bf16[4,2,128,256]{3,2,1,0:T(8,128)(2,1)S(1)}, bf16[4,2,128,256]{3,2,1,0:T(8,128)(2,1)S(1)}, bf16[4,2,128,256]{3,2,1,0:T(8,128)(2,1)S(1)}) fusion(f32[4,4,2,128,256]{4,3,2,1,0:T(8,128)} %bitcast.72, s32[]{:T(128)S(6)} %select_n.177, s32[]{:T(128)S(6)} %select_n.181, s32[]{:T(128)S(6)} %select_n.179), kind=kLoop, calls=%fused_computation.13 | loop fusion | bytes 3145740 | tf_op jit(solution)/shard_map/convert_element_type | solution.py:161
  53.3 4.8 %collective-permute-start.8 = (bf16[4,2,128,256]{3,2,1,0:T(8,128)(2,1)S(1)}, bf16[4,2,128,256]{3,2,1,0:T(8,128)(2,1)S(1)}, u32[]{:S(2)}, u32[]{:S(2)}) collective-permute-start(bf16[4,2,128,256]{3,2,1,0:T(8,128)(2,1)S(1)} %get-tuple-element.19), channel_id=1, source_target_pairs={{0,6},{2,0},{4,2},{6,4},{1,7},{3,1},{5,3},{7,5},{8,14},{10,8},{12,... | collective-permute-start | bytes 1572872 | tf_op jit(solution)/shard_map/ppermute | solution.py:149
  58.1 0.6 collective-permute-start.6
  58.7 11.7 %collective-permute-done.8 = bf16[4,2,128,256]{3,2,1,0:T(8,128)(2,1)S(1)} collective-permute-done((bf16[4,2,128,256]{3,2,1,0:T(8,128)(2,1)S(1)}, bf16[4,2,128,256]{3,2,1,0:T(8,128)(2,1)S(1)}, u32[]{:S(2)}, u32[]{:S(2)}) %collective-permute-start.8) | collective-permute-done | bytes 524320 | tf_op jit(solution)/shard_map/ppermute | solution.py:149
  70.4 8.6 %collective-permute-done.7 = bf16[4,2,128,256]{3,2,1,0:T(8,128)(2,1)S(1)} collective-permute-done((bf16[4,2,128,256]{3,2,1,0:T(8,128)(2,1)S(1)}, bf16[4,2,128,256]{3,2,1,0:T(8,128)(2,1)S(1)}, u32[]{:S(2)}, u32[]{:S(2)}) %collective-permute-start.7) | collective-permute-done | bytes 524320 | tf_op jit(solution)/shard_map/ppermute | solution.py:149
  79.0 1.8 %collective-permute-done.6 = bf16[4,2,128,256]{3,2,1,0:T(8,128)(2,1)S(1)} collective-permute-done((bf16[4,2,128,256]{3,2,1,0:T(8,128)(2,1)S(1)}, bf16[4,2,128,256]{3,2,1,0:T(8,128)(2,1)S(1)}, u32[]{:S(2)}, u32[]{:S(2)}) %collective-permute-start.6) | collective-permute-done | bytes 524320 | tf_op jit(solution)/shard_map/ppermute | solution.py:149
  80.9 1.4 %fusion.1 = f32[4,2,128,256]{3,2,1,0:T(8,128)S(1)} fusion(bf16[4,2,128,256]{3,2,1,0:T(8,128)(2,1)S(1)} %collective-permute-done.8, bf16[4,2,128,256]{3,2,1,0:T(8,128)(2,1)S(1)} %collective-permute-done.7, bf16[4,2,128,256]{3,2,1,0:T(8,128)(2,1)S(1)} %collective-permute-done.6, f32[4,4,2,128,256]{4,3,2,1,0:T(8,128)} %bitcast.73, s32[]{:T(128)S(6)} %select_n.175), kind=kLoop, calls=%fused_computation.9 | loop fusion | flops 1572864 | bytes 3670020 | tf_op jit(solution)/shard_map/add | solution.py:161
  82.4 12.5 %collective-permute-start.11 = (bf16[2,128,256]{2,1,0:T(8,128)(2,1)S(1)}, bf16[2,128,256]{2,1,0:T(8,128)(2,1)S(1)}, u32[]{:S(2)}, u32[]{:S(2)}) collective-permute-start(bf16[2,128,256]{2,1,0:T(8,128)(2,1)S(1)} %get-tuple-element.22), channel_id=1, source_target_pairs={{0,24},{8,0},{16,8},{24,16},{1,25},{9,1},{17,9},{25,17},{2,26},{10... | collective-permute-start | bytes 393224 | tf_op jit(solution)/shard_map/ppermute | solution.py:149
  94.9 2.3 %collective-permute-start.10 = (bf16[2,128,256]{2,1,0:T(8,128)(2,1)S(1)}, bf16[2,128,256]{2,1,0:T(8,128)(2,1)S(1)}, u32[]{:S(2)}, u32[]{:S(2)}) collective-permute-start(bf16[2,128,256]{2,1,0:T(8,128)(2,1)S(1)} %get-tuple-element.23), channel_id=1, source_target_pairs={{0,16},{8,24},{16,0},{24,8},{1,17},{9,25},{17,1},{25,9},{2,18},{10... | collective-permute-start | bytes 393224 | tf_op jit(solution)/shard_map/ppermute | solution.py:149
  97.2 1.9 %collective-permute-start.9 = (bf16[2,128,256]{2,1,0:T(8,128)(2,1)S(1)}, bf16[2,128,256]{2,1,0:T(8,128)(2,1)S(1)}, u32[]{:S(2)}, u32[]{:S(2)}) collective-permute-start(bf16[2,128,256]{2,1,0:T(8,128)(2,1)S(1)} %get-tuple-element.21), channel_id=1, source_target_pairs={{0,8},{8,16},{16,24},{24,0},{1,9},{9,17},{17,25},{25,1},{2,10},{10... | collective-permute-start | bytes 393224 | tf_op jit(solution)/shard_map/ppermute | solution.py:149
  99.1 9.2 %collective-permute-done.10 = bf16[2,128,256]{2,1,0:T(8,128)(2,1)S(1)} collective-permute-done((bf16[2,128,256]{2,1,0:T(8,128)(2,1)S(1)}, bf16[2,128,256]{2,1,0:T(8,128)(2,1)S(1)}, u32[]{:S(2)}, u32[]{:S(2)}) %collective-permute-start.10) | collective-permute-done | bytes 131104 | tf_op jit(solution)/shard_map/ppermute | solution.py:149
  108.4 0.7 fusion.32
  (23 shorter events, 0.2 us)
Async XLA Ops:
  0.6 11.4 %copy-start.2 = (s32[64]{0:T(128)S(1)}, s32[64]{0:T(128)}, u32[]{:S(2)}) copy-start(s32[64]{0:T(128)} %param.15) | copy-start | bytes 772
  2.4 11.2 %collective-permute-start.2 = (bf16[256,256]{1,0:T(8,128)(2,1)S(1)}, bf16[256,256]{1,0:T(8,128)(2,1)S(1)}, u32[]{:S(2)}, u32[]{:S(2)}) collective-permute-start(bf16[256,256]{1,0:T(8,128)(2,1)S(1)} %constant_dynamic-update-slice_fusion), channel_id=1, source_target_pairs={{0,24},{8,0},{16,8},{24,16},{1,25},{9,1},{17,9},{25,17},{2,26},{10... | collective-permute-start | bytes 393224 | tf_op jit(solution)/shard_map/ppermute | solution.py:149
  7.5 11.2 %collective-permute-start.1 = (bf16[256,256]{1,0:T(8,128)(2,1)S(1)}, bf16[256,256]{1,0:T(8,128)(2,1)S(1)}, u32[]{:S(2)}, u32[]{:S(2)}) collective-permute-start(bf16[256,256]{1,0:T(8,128)(2,1)S(1)} %constant_dynamic-update-slice_fusion), channel_id=1, source_target_pairs={{0,16},{8,24},{16,0},{24,8},{1,17},{9,25},{17,1},{25,9},{2,18},{10... | collective-permute-start | bytes 393224 | tf_op jit(solution)/shard_map/ppermute | solution.py:149
  7.5 11.2 %collective-permute-start = (bf16[256,256]{1,0:T(8,128)(2,1)S(1)}, bf16[256,256]{1,0:T(8,128)(2,1)S(1)}, u32[]{:S(2)}, u32[]{:S(2)}) collective-permute-start(bf16[256,256]{1,0:T(8,128)(2,1)S(1)} %constant_dynamic-update-slice_fusion), channel_id=1, source_target_pairs={{0,8},{8,16},{16,24},{24,0},{1,9},{9,17},{17,25},{25,1},{2,10},{10... | collective-permute-start | bytes 393224 | tf_op jit(solution)/shard_map/ppermute | solution.py:149
  11.5 14.0 %copy-start = (s32[16,3,8]{2,1,0:T(4,128)S(1)}, s32[16,3,8]{2,1,0:T(4,128)}, u32[]{:S(2)}) copy-start(s32[16,3,8]{2,1,0:T(4,128)} %constant.145.clone) | copy-start | bytes 4612
  18.8 20.6 %copy-start.1 = (bf16[4,256,256]{2,1,0:T(8,128)(2,1)}, bf16[4,256,256]{2,1,0:T(8,128)(2,1)S(1)}, u32[]{:S(2)}) copy-start(bf16[4,256,256]{2,1,0:T(8,128)(2,1)S(1)} %pad_maximum_fusion) | copy-start | bytes 1572868
  19.5 13.0 %collective-permute-start.3 = (bf16[6,128,256]{2,1,0:T(8,128)(2,1)S(1)}, bf16[6,128,256]{2,1,0:T(8,128)(2,1)S(1)}, u32[]{:S(2)}, u32[]{:S(2)}) collective-permute-start(bf16[6,128,256]{2,1,0:T(8,128)(2,1)S(1)} %broadcast_select_fusion.2), channel_id=1, source_target_pairs={{0,2},{2,4},{4,6},{6,0},{1,3},{3,5},{5,7},{7,1},{8,10},{10,12},{12... | collective-permute-start | bytes 1179656 | tf_op jit(solution)/shard_map/ppermute | solution.py:149
  21.7 17.6 %collective-permute-start.4 = (bf16[6,128,256]{2,1,0:T(8,128)(2,1)S(1)}, bf16[6,128,256]{2,1,0:T(8,128)(2,1)S(1)}, u32[]{:S(2)}, u32[]{:S(2)}) collective-permute-start(bf16[6,128,256]{2,1,0:T(8,128)(2,1)S(1)} %broadcast_select_fusion.1), channel_id=1, source_target_pairs={{0,4},{2,6},{4,0},{6,2},{1,5},{3,7},{5,1},{7,3},{8,12},{10,14},{12... | collective-permute-start | bytes 1179656 | tf_op jit(solution)/shard_map/ppermute | solution.py:149
  24.0 15.4 %collective-permute-start.5 = (bf16[6,128,256]{2,1,0:T(8,128)(2,1)S(1)}, bf16[6,128,256]{2,1,0:T(8,128)(2,1)S(1)}, u32[]{:S(2)}, u32[]{:S(2)}) collective-permute-start(bf16[6,128,256]{2,1,0:T(8,128)(2,1)S(1)} %broadcast_select_fusion), channel_id=1, source_target_pairs={{0,6},{2,0},{4,2},{6,4},{1,7},{3,1},{5,3},{7,5},{8,14},{10,8},{12,... | collective-permute-start | bytes 1179656 | tf_op jit(solution)/shard_map/ppermute | solution.py:149
  32.5 6.9 %copy-start.3 = (bf16[6,128,256]{2,1,0:T(8,128)(2,1)}, bf16[6,128,256]{2,1,0:T(8,128)(2,1)S(1)}, u32[]{:S(2)}) copy-start(bf16[6,128,256]{2,1,0:T(8,128)(2,1)S(1)} %collective-permute-done.3) | copy-start | bytes 1179652
  39.3 0.8 copy-start.4
  39.4 0.8 copy-start.5
  53.3 17.1 %collective-permute-start.8 = (bf16[4,2,128,256]{3,2,1,0:T(8,128)(2,1)S(1)}, bf16[4,2,128,256]{3,2,1,0:T(8,128)(2,1)S(1)}, u32[]{:S(2)}, u32[]{:S(2)}) collective-permute-start(bf16[4,2,128,256]{3,2,1,0:T(8,128)(2,1)S(1)} %get-tuple-element.19), channel_id=1, source_target_pairs={{0,6},{2,0},{4,2},{6,4},{1,7},{3,1},{5,3},{7,5},{8,14},{10,8},{12,... | collective-permute-start | bytes 1572872 | tf_op jit(solution)/shard_map/ppermute | solution.py:149
  58.1 21.0 %collective-permute-start.7 = (bf16[4,2,128,256]{3,2,1,0:T(8,128)(2,1)S(1)}, bf16[4,2,128,256]{3,2,1,0:T(8,128)(2,1)S(1)}, u32[]{:S(2)}, u32[]{:S(2)}) collective-permute-start(bf16[4,2,128,256]{3,2,1,0:T(8,128)(2,1)S(1)} %get-tuple-element.20), channel_id=1, source_target_pairs={{0,4},{2,6},{4,0},{6,2},{1,5},{3,7},{5,1},{7,3},{8,12},{10,14},{12... | collective-permute-start | bytes 1572872 | tf_op jit(solution)/shard_map/ppermute | solution.py:149
  58.1 22.7 %collective-permute-start.6 = (bf16[4,2,128,256]{3,2,1,0:T(8,128)(2,1)S(1)}, bf16[4,2,128,256]{3,2,1,0:T(8,128)(2,1)S(1)}, u32[]{:S(2)}, u32[]{:S(2)}) collective-permute-start(bf16[4,2,128,256]{3,2,1,0:T(8,128)(2,1)S(1)} %get-tuple-element.18), channel_id=1, source_target_pairs={{0,2},{2,4},{4,6},{6,0},{1,3},{3,5},{5,7},{7,1},{8,10},{10,12},{12... | collective-permute-start | bytes 1572872 | tf_op jit(solution)/shard_map/ppermute | solution.py:149
  82.4 16.7 %collective-permute-start.11 = (bf16[2,128,256]{2,1,0:T(8,128)(2,1)S(1)}, bf16[2,128,256]{2,1,0:T(8,128)(2,1)S(1)}, u32[]{:S(2)}, u32[]{:S(2)}) collective-permute-start(bf16[2,128,256]{2,1,0:T(8,128)(2,1)S(1)} %get-tuple-element.22), channel_id=1, source_target_pairs={{0,24},{8,0},{16,8},{24,16},{1,25},{9,1},{17,9},{25,17},{2,26},{10... | collective-permute-start | bytes 393224 | tf_op jit(solution)/shard_map/ppermute | solution.py:149
  94.9 13.5 %collective-permute-start.10 = (bf16[2,128,256]{2,1,0:T(8,128)(2,1)S(1)}, bf16[2,128,256]{2,1,0:T(8,128)(2,1)S(1)}, u32[]{:S(2)}, u32[]{:S(2)}) collective-permute-start(bf16[2,128,256]{2,1,0:T(8,128)(2,1)S(1)} %get-tuple-element.23), channel_id=1, source_target_pairs={{0,16},{8,24},{16,0},{24,8},{1,17},{9,25},{17,1},{25,9},{2,18},{10... | collective-permute-start | bytes 393224 | tf_op jit(solution)/shard_map/ppermute | solution.py:149
  97.2 11.2 %collective-permute-start.9 = (bf16[2,128,256]{2,1,0:T(8,128)(2,1)S(1)}, bf16[2,128,256]{2,1,0:T(8,128)(2,1)S(1)}, u32[]{:S(2)}, u32[]{:S(2)}) collective-permute-start(bf16[2,128,256]{2,1,0:T(8,128)(2,1)S(1)} %get-tuple-element.21), channel_id=1, source_target_pairs={{0,8},{8,16},{16,24},{24,0},{1,9},{9,17},{17,25},{25,1},{2,10},{10... | collective-permute-start | bytes 393224 | tf_op jit(solution)/shard_map/ppermute | solution.py:149

commit v4 on v3

--- a/solution.py
+++ b/solution.py
@@ -143,6 +143,51 @@
         for i, e in enumerate(got):
             where[sr, k - 1, e] = i
     return most, send, where
+
+
+def _partial_tables(n_seq, n_out, n_in, reach):
+    def needs(dp, d, slot):
+        j = d if slot == 0 else 2 * n_seq - 1 - d
+        up = 2 * n_seq - 1 - dp
+        return (dp - reach <= j <= dp) or (up - reach <= j <= up)
+
+    lists = {}
+    for sr in range(n_seq):
+        zs, ws = divmod(sr, n_in)
+        for k in range(1, n_in):
+            wr = (ws + k) % n_in
+            lists[sr, k] = [
+                e for e in range(2 * n_out) if needs(sr, (e // 2) * n_in + wr, e % 2)
+            ]
+    most = max(len(v) for v in lists.values())
+    send = np.zeros((n_seq, n_in - 1, most), np.int32)
+    where = np.full((n_seq, n_in - 1, 2 * n_out), -1, np.int32)
+    for (sr, k), got in lists.items():
+        send[sr, k - 1] = got + [got[0] if got else 0] * (most - len(got))
+        for i, e in enumerate(got):
+            where[sr, k - 1, e] = i
+    return most, send, where
+
+
+def _plane_reduce(storage, rank, n_seq, n_out, n_in, reach):
+    most, send_np, where_np = _partial_tables(n_seq, n_out, n_in, reach)
+    me_w = lax.axis_index("w")
+    me_z = lax.axis_index("zp")
+    send_tab = jnp.asarray(send_np)[rank]
+    where_tab = jnp.asarray(where_np)
+    block = storage.shape[3:]
+    total = lax.dynamic_index_in_dim(storage, me_w, 1, keepdims=False)
+    total = total.reshape((2 * n_out,) + block)
+    for k in range(1, n_in):
+        piece = lax.dynamic_index_in_dim(storage, (me_w + k) % n_in, 1, keepdims=False)
+        piece = piece.reshape((2 * n_out,) + block)
+        chosen = jnp.take(piece, send_tab[k - 1], axis=0).astype(jnp.bfloat16)
+        got = _shift(chosen, k, n_in, "w")
+        sender = me_z * n_in + (me_w - k) % n_in
+        pos = where_tab[sender, k - 1]
+        picked = jnp.take(got, jnp.maximum(pos, 0), axis=0).astype(jnp.float32)
+        total = total + jnp.where((pos >= 0)[:, None, None], picked, 0.0)
+    return total.reshape((n_out, 2) + block)
 
 
 def _shift(x, k, n, axis):
@@ -251,7 +296,7 @@
 
     storage = partial
     storage = storage.reshape(n_out, n_in, 2, rows, 2 * width)
-    plane = _group_reduce(storage, n_in, "w", 1)
+    plane = _plane_reduce(storage, rank, n_seq, n_out, n_in, REACH)
     summed = _group_reduce(plane, n_out, "zp", 0).reshape(2 * rows, 2 * width)
     grad_keys = summed[:, :width].astype(jnp.bfloat16)
     grad_values = summed[:, width:].astype(jnp.bfloat16)

time: 110 us -> 103 us (0.936); the launches traced: 109 us -> 101 us
  waiting for transfers between devices: 48.6 us -> 32 us
  local copies, waits for them, and re-layouts: 10.1 us -> 16.3 us
  other arithmetic: 5.67 us -> 9.25 us
  starting transfers between devices: 32.9 us -> 31.4 us
    ppermute x12, waiting for transfers between devices: 48.6 us -> 32 us  [_shift(): return lax.ppermute(x, axis, [(i, (i + k) % n) for i in range(n)])]
    gather x0 -> x6, local copies, waits for them, and re-layouts: none -> 4.25 us  [the longest x3 2.54 us: _plane_reduce(): picked = jnp.take(got, jnp.maximum(pos, 0), axis=0).astype(jnp.float32)]
    dynamic_slice x0 -> x3, local copies, waits for them, and re-layouts: none -> 4.1 us  [the longest x1 2.08 us: _plane_reduce(): lax.dynamic_index_in_dim(storage, (me_w + k) % n_in, 1, keepdims=False)]
    convert_element_type x2 -> x1, local copies, waits for them, and re-layouts: 2.13 us -> 0.05 us  [_group_reduce(): piece.astype(jnp.bfloat16)]
    ppermute x12, starting transfers between devices: 32.9 us -> 31.4 us  [_shift(): return lax.ppermute(x, axis, [(i, (i + k) % n) for i in range(n)])]
    convert_element_type x0 -> x3, other arithmetic: none -> 1.24 us  [_plane_reduce(): chosen = jnp.take(piece, send_tab[k - 1], axis=0).astype(jnp.bfloat16)]
    ge x0 -> x1, other arithmetic: none -> 1.23 us  [_plane_reduce(): total = total + jnp.where((pos >= 0)[:, None, None], picked, 0.0)]
  transfers between devices with their start and end apart: 12 -> 12, of which waited for: 8 -> 8; matrix products, arithmetic and copies ran while one was open for 7% -> 15% of each run, Pallas kernels for 0% -> 0%
where the time goes in v4:
time: 103 us; the launch traced here: 101 us
  waiting for transfers between devices  32 us (31%)
  starting transfers between devices  31.4 us (30%)
  local copies, waits for them, and re-layouts  16.3 us (16%)
  Pallas kernels  11 us (11%)
  other arithmetic  9.25 us (9%)
    ppermute x12, waiting for transfers between devices, _shift(): return lax.ppermute(x, axis, [(i, (i + k) % n) for i in range(n)])  32 us
    ppermute x12, starting transfers between devices, _shift(): return lax.ppermute(x, axis, [(i, (i + k) % n) for i in range(n)])  31.4 us
    pallas_call x1, Pallas kernels, body(): pl.pallas_call(kernel, grid_spec=grid_spec, out_shape=[jax.ShapeDtypeStru...  11 us
    gather x3, local copies, waits for them, and re-layouts, _plane_reduce(): picked = jnp.take(got, jnp.maximum(pos, 0), axis=0).astype(jnp.float32)  2.54 us
    dynamic_slice x1, local copies, waits for them, and re-layouts, _plane_reduce(): lax.dynamic_index_in_dim(storage, (me_w + k) % n_in, 1, keepdims=False)  2.08 us
  transfers between devices with their start and end apart: 12, of which 8 were waited for; matrix products, arithmetic and copies ran while one was open for 15% of the time, Pallas kernels for 0%

profile of v4, /device:TPU:0, one launch (start us, length us, event | category | flops | bytes accessed | tf_op | source)
XLA Modules:
  0.0 100.9 jit_solution(10116879304877575856)
XLA Ops:
  0.7 0.9 constant_dynamic-update-slice_fusion.1
  1.5 0.9 constant_dynamic-update-slice_fusion
  2.4 3.1 %collective-permute-start = (bf16[256,256]{1,0:T(8,128)(2,1)S(1)}, bf16[256,256]{1,0:T(8,128)(2,1)S(1)}, u32[]{:S(2)}, u32[]{:S(2)}) collective-permute-start(bf16[256,256]{1,0:T(8,128)(2,1)S(1)} %constant_dynamic-update-slice_fusion), channel_id=1, source_target_pairs={{0,8},{8,16},{16,24},{24,0},{1,9},{9,17},{17,25},{25,1},{2,10},{10... | collective-permute-start | bytes 393224 | tf_op jit(solution)/shard_map/ppermute | solution.py:194
  5.5 2.6 %collective-permute-start.1 = (bf16[256,256]{1,0:T(8,128)(2,1)S(1)}, bf16[256,256]{1,0:T(8,128)(2,1)S(1)}, u32[]{:S(2)}, u32[]{:S(2)}) collective-permute-start(bf16[256,256]{1,0:T(8,128)(2,1)S(1)} %constant_dynamic-update-slice_fusion), channel_id=1, source_target_pairs={{0,16},{8,24},{16,0},{24,8},{1,17},{9,25},{17,1},{25,9},{2,18},{10... | collective-permute-start | bytes 393224 | tf_op jit(solution)/shard_map/ppermute | solution.py:194
  8.1 1.3 %collective-permute-start.2 = (bf16[256,256]{1,0:T(8,128)(2,1)S(1)}, bf16[256,256]{1,0:T(8,128)(2,1)S(1)}, u32[]{:S(2)}, u32[]{:S(2)}) collective-permute-start(bf16[256,256]{1,0:T(8,128)(2,1)S(1)} %constant_dynamic-update-slice_fusion), channel_id=1, source_target_pairs={{0,24},{8,0},{16,8},{24,16},{1,25},{9,1},{17,9},{25,17},{2,26},{10... | collective-permute-start | bytes 393224 | tf_op jit(solution)/shard_map/ppermute | solution.py:194
  9.4 0.7 constant_dynamic-slice_fusion.4
  10.1 0.7 constant_dynamic-slice_fusion.8
  10.9 0.6 broadcast_add_fusion
  11.7 1.4 %multiply_bitcast_fusion = f32[32,8,8,128]{3,1,2,0:T(8,128)S(1)} fusion(bf16[256,1024]{1,0:T(8,128)(2,1)} %param.19, bf16[256,1024]{1,0:T(8,128)(2,1)} %do_ref.1), kind=kLoop, calls=%fused_computation.14 | loop fusion | flops 786432 | bytes 2097152
  13.0 0.2 copy.17
  13.2 0.3 bitcast_reduce_fusion
  13.7 0.7 copy.16
  14.7 0.5 sub.90.starts_ref
  15.2 1.2 %gather_fusion = s32[34]{0:T(128)S(1)} fusion(s32[16,3,8]{2,1,0:T(4,128)S(1)} %copy-done, s32[34]{0:T(128)S(1)} %fusion.28), kind=kCustom, calls=%fused_computation.9 | custom fusion | bytes 680 | tf_op jit(solution)/shard_map/gather | solution.py:244
  16.4 0.3 collective-permute-done.1
  16.8 0.6 gather_fusion.2
  17.5 1.6 %collective-permute-start.4 = (bf16[6,128,256]{2,1,0:T(8,128)(2,1)S(1)}, bf16[6,128,256]{2,1,0:T(8,128)(2,1)S(1)}, u32[]{:S(2)}, u32[]{:S(2)}) collective-permute-start(bf16[6,128,256]{2,1,0:T(8,128)(2,1)S(1)} %broadcast_select_fusion.1), channel_id=1, source_target_pairs={{0,4},{2,6},{4,0},{6,2},{1,5},{3,7},{5,1},{7,3},{8,12},{10,14},{12... | collective-permute-start | bytes 1179656 | tf_op jit(solution)/shard_map/ppermute | solution.py:194
  19.1 0.6 gather_fusion.3
  19.8 1.5 %collective-permute-start.5 = (bf16[6,128,256]{2,1,0:T(8,128)(2,1)S(1)}, bf16[6,128,256]{2,1,0:T(8,128)(2,1)S(1)}, u32[]{:S(2)}, u32[]{:S(2)}) collective-permute-start(bf16[6,128,256]{2,1,0:T(8,128)(2,1)S(1)} %broadcast_select_fusion), channel_id=1, source_target_pairs={{0,6},{2,0},{4,2},{6,4},{1,7},{3,1},{5,3},{7,5},{8,14},{10,8},{12,... | collective-permute-start | bytes 1179656 | tf_op jit(solution)/shard_map/ppermute | solution.py:194
  21.3 0.6 gather_fusion.1
  21.9 0.6 collective-permute-start.3
  22.6 0.7 compare_and_fusion.4
  23.3 0.6 fusion.9
  23.9 4.6 %collective-permute-done.4 = bf16[6,128,256]{2,1,0:T(8,128)(2,1)S(1)} collective-permute-done((bf16[6,128,256]{2,1,0:T(8,128)(2,1)S(1)}, bf16[6,128,256]{2,1,0:T(8,128)(2,1)S(1)}, u32[]{:S(2)}, u32[]{:S(2)}) %collective-permute-start.4) | collective-permute-done | bytes 393248 | tf_op jit(solution)/shard_map/ppermute | solution.py:194
  28.5 3.3 %collective-permute-done.5 = bf16[6,128,256]{2,1,0:T(8,128)(2,1)S(1)} collective-permute-done((bf16[6,128,256]{2,1,0:T(8,128)(2,1)S(1)}, bf16[6,128,256]{2,1,0:T(8,128)(2,1)S(1)}, u32[]{:S(2)}, u32[]{:S(2)}) %collective-permute-start.5) | collective-permute-done | bytes 393248 | tf_op jit(solution)/shard_map/ppermute | solution.py:194
  31.8 7.0 %collective-permute-done.3 = bf16[6,128,256]{2,1,0:T(8,128)(2,1)S(1)} collective-permute-done((bf16[6,128,256]{2,1,0:T(8,128)(2,1)S(1)}, bf16[6,128,256]{2,1,0:T(8,128)(2,1)S(1)}, u32[]{:S(2)}, u32[]{:S(2)}) %collective-permute-start.3) | collective-permute-done | bytes 393248 | tf_op jit(solution)/shard_map/ppermute | solution.py:194
  38.9 0.7 copy-done.5
  39.6 11.0 %shard_map.121 = (bf16[256,1024]{1,0:T(8,128)(2,1)}, f32[32,128,256]{2,1,0:T(8,128)}) custom-call(s32[2]{0:T(128)} %get-tuple-element.31.blk_ref, s32[64]{0:T(128)} %sub.90.starts_ref, s32[34]{0:T(128)} %get-tuple-element.28.srow_ref, s32[34]{0:T(128)} %get-tuple-element.29.src_ref, s32[34]{0:T(128)} %get-tuple-element.55.dst_ref, bf16[256,1024]{1,0:T(8,128)(2,1)} %q_ref.1, ...), custom_call_target="tpu_custom_call" | custom-call | flops 6845104128 | bytes 8388608 | tf_op jit(solution)/shard_map/pallas_call | solution.py:283
  50.6 2.1 %constant_dynamic-slice_fusion.5 = (bf16[4,1,2,128,256]{4,3,2,1,0:T(8,128)(2,1)S(1)}, bf16[4,1,2,128,256]{4,3,2,1,0:T(8,128)(2,1)S(1)}, bf16[4,1,2,128,256]{4,3,2,1,0:T(8,128)(2,1)S(1)}) fusion(f32[4,4,2,128,256]{4,3,2,1,0:T(8,128)} %bitcast.88, s32[]{:T(128)S(6)} %select_n.224, s32[]{:T(128)S(6)} %select_n.234, s32[]{:T(128)S(6)} %select_n.229), kind=kLoop, calls=%fused_computation.48 | loop fusion | bytes 3145740 | tf_op jit(solution)/shard_map/jit(dynamic_index_in_dim)/dynamic_slice | solution.py:182
  52.7 0.6 gather_fusion.6
  53.5 13.2 %collective-permute-start.7 = (bf16[6,128,256]{2,1,0:T(8,128)(2,1)S(1)}, bf16[6,128,256]{2,1,0:T(8,128)(2,1)S(1)}, u32[]{:S(2)}, u32[]{:S(2)}) collective-permute-start(bf16[6,128,256]{2,1,0:T(8,128)(2,1)S(1)} %select_convert_fusion.1), channel_id=1, source_target_pairs={{0,4},{2,6},{4,0},{6,2},{1,5},{3,7},{5,1},{7,3},{8,12},{10,14},{12... | collective-permute-start | bytes 1179656 | tf_op jit(solution)/shard_map/ppermute | solution.py:194
  66.7 0.6 gather_fusion.4
  67.4 0.9 collective-permute-start.6
  68.4 0.6 gather_fusion.8
  69.0 0.9 select_convert_fusion
  69.9 2.0 %collective-permute-start.8 = (bf16[6,128,256]{2,1,0:T(8,128)(2,1)}, bf16[6,128,256]{2,1,0:T(8,128)(2,1)S(1)}, u32[]{:S(2)}, u32[]{:S(2)}) collective-permute-start(bf16[6,128,256]{2,1,0:T(8,128)(2,1)} %select_convert_fusion), channel_id=1, source_target_pairs={{0,6},{2,0},{4,2},{6,4},{1,7},{3,1},{5,3},{7,5},{8,14},{10,8},{12,... | collective-permute-start | bytes 1179656 | tf_op jit(solution)/shard_map/ppermute | solution.py:194
  71.9 1.2 %compare_bitcast_fusion.2 = (pred[8]{0:T(512)(128)(4,1)S(1)}, pred[8]{0:T(512)(128)(4,1)}, pred[8]{0:T(512)(128)(4,1)}) fusion(s32[16,3,8]{2,1,0:T(4,128)} %constant.189.clone, s32[]{:T(128)S(6)} %select_n.222, s32[]{:T(128)S(6)} %select_n.232, s32[]{:T(128)S(6)} %select_n.227), kind=kLoop, calls=%fused_computation.84 | loop fusion | flops 24 | bytes 132 | tf_op jit(solution)/shard_map/ge | solution.py:189
  73.2 1.3 %constant_dynamic-slice_fusion.7 = f32[4,1,2,128,256]{4,3,2,1,0:T(8,128)S(1)} fusion(f32[4,4,2,128,256]{4,3,2,1,0:T(8,128)} %bitcast.89, s32[]{:T(128)S(6)} %select_n.220), kind=kLoop, calls=%fused_computation.50 | loop fusion | bytes 2097156 | tf_op jit(solution)/shard_map/jit(dynamic_index_in_dim)/dynamic_slice | solution.py:179
  74.5 8.7 %collective-permute-done.7 = bf16[6,128,256]{2,1,0:T(8,128)(2,1)S(1)} collective-permute-done((bf16[6,128,256]{2,1,0:T(8,128)(2,1)S(1)}, bf16[6,128,256]{2,1,0:T(8,128)(2,1)S(1)}, u32[]{:S(2)}, u32[]{:S(2)}) %collective-permute-start.7) | collective-permute-done | bytes 393248 | tf_op jit(solution)/shard_map/ppermute | solution.py:194
  83.2 0.6 gather_fusion.7
  83.8 0.6 gather_fusion.5
  84.4 0.8 collective-permute-done.8
  85.2 1.4 %gather_fusion.9 = bf16[8,128,256]{2,1,0:T(8,128)(2,1)} fusion(bf16[6,128,256]{2,1,0:T(8,128)(2,1)S(1)} %collective-permute-done.8, s32[1024]{0:T(1024)S(1)} %get-tuple-element.62), kind=kCustom, calls=%fused_computation.8.clone | custom fusion | bytes 1048608 | tf_op jit(solution)/shard_map/jit(_take)/gather | solution.py:188
  86.6 1.8 %fusion.1 = f32[8,128,256]{2,1,0:T(8,128)S(1)} fusion(f32[4,1,2,128,256]{4,3,2,1,0:T(8,128)S(1)} %constant_dynamic-slice_fusion.7, bf16[8,128,256]{2,1,0:T(8,128)(2,1)} %gather_fusion.9, bf16[8,128,256]{2,1,0:T(8,128)(2,1)S(1)} %gather_fusion.7, bf16[8,128,256]{2,1,0:T(8,128)(2,1)S(1)} %gather_fusion.5, pred[8]{0:T(512)(128)(4,1)S(1)} %get-tuple-element.43, ...), kind=kLoop, calls=%fused_computation.13 | loop fusion | flops 3145728 | bytes 3670064 | tf_op jit(solution)/shard_map/add | solution.py:189
  88.5 4.3 %collective-permute-start.11 = (bf16[2,128,256]{2,1,0:T(8,128)(2,1)S(1)}, bf16[2,128,256]{2,1,0:T(8,128)(2,1)S(1)}, u32[]{:S(2)}, u32[]{:S(2)}) collective-permute-start(bf16[2,128,256]{2,1,0:T(8,128)(2,1)S(1)} %get-tuple-element.36), channel_id=1, source_target_pairs={{0,24},{8,0},{16,8},{24,16},{1,25},{9,1},{17,9},{25,17},{2,26},{10... | collective-permute-start | bytes 393224 | tf_op jit(solution)/shard_map/ppermute | solution.py:194
  92.9 5.6 %collective-permute-done.10 = bf16[2,128,256]{2,1,0:T(8,128)(2,1)S(1)} collective-permute-done((bf16[2,128,256]{2,1,0:T(8,128)(2,1)S(1)}, bf16[2,128,256]{2,1,0:T(8,128)(2,1)S(1)}, u32[]{:S(2)}, u32[]{:S(2)}) %collective-permute-start.10) | collective-permute-done | bytes 131104 | tf_op jit(solution)/shard_map/ppermute | solution.py:194
  98.5 1.7 %collective-permute-done.9 = bf16[2,128,256]{2,1,0:T(8,128)(2,1)S(1)} collective-permute-done((bf16[2,128,256]{2,1,0:T(8,128)(2,1)S(1)}, bf16[2,128,256]{2,1,0:T(8,128)(2,1)S(1)}, u32[]{:S(2)}, u32[]{:S(2)}) %collective-permute-start.9) | collective-permute-done | bytes 131104 | tf_op jit(solution)/shard_map/ppermute | solution.py:194
  100.2 0.7 fusion.29
  (41 shorter events, 1.6 us)
Async XLA Ops:
  0.6 14.6 %copy-start = (s32[16,3,8]{2,1,0:T(4,128)S(1)}, s32[16,3,8]{2,1,0:T(4,128)}, u32[]{:S(2)}) copy-start(s32[16,3,8]{2,1,0:T(4,128)} %constant.187.clone) | copy-start | bytes 4612
  0.6 13.7 %copy-start.2 = (s32[64]{0:T(128)S(1)}, s32[64]{0:T(128)}, u32[]{:S(2)}) copy-start(s32[64]{0:T(128)} %param.21) | copy-start | bytes 772
  2.4 14.0 %collective-permute-start = (bf16[256,256]{1,0:T(8,128)(2,1)S(1)}, bf16[256,256]{1,0:T(8,128)(2,1)S(1)}, u32[]{:S(2)}, u32[]{:S(2)}) collective-permute-start(bf16[256,256]{1,0:T(8,128)(2,1)S(1)} %constant_dynamic-update-slice_fusion), channel_id=1, source_target_pairs={{0,8},{8,16},{16,24},{24,0},{1,9},{9,17},{17,25},{25,1},{2,10},{10... | collective-permute-start | bytes 393224 | tf_op jit(solution)/shard_map/ppermute | solution.py:194
  5.5 11.2 %collective-permute-start.1 = (bf16[256,256]{1,0:T(8,128)(2,1)S(1)}, bf16[256,256]{1,0:T(8,128)(2,1)S(1)}, u32[]{:S(2)}, u32[]{:S(2)}) collective-permute-start(bf16[256,256]{1,0:T(8,128)(2,1)S(1)} %constant_dynamic-update-slice_fusion), channel_id=1, source_target_pairs={{0,16},{8,24},{16,0},{24,8},{1,17},{9,25},{17,1},{25,9},{2,18},{10... | collective-permute-start | bytes 393224 | tf_op jit(solution)/shard_map/ppermute | solution.py:194
  8.1 8.6 %collective-permute-start.2 = (bf16[256,256]{1,0:T(8,128)(2,1)S(1)}, bf16[256,256]{1,0:T(8,128)(2,1)S(1)}, u32[]{:S(2)}, u32[]{:S(2)}) collective-permute-start(bf16[256,256]{1,0:T(8,128)(2,1)S(1)} %constant_dynamic-update-slice_fusion), channel_id=1, source_target_pairs={{0,24},{8,0},{16,8},{24,16},{1,25},{9,1},{17,9},{25,17},{2,26},{10... | collective-permute-start | bytes 393224 | tf_op jit(solution)/shard_map/ppermute | solution.py:194
  16.8 22.1 %copy-start.1 = (bf16[4,256,256]{2,1,0:T(8,128)(2,1)}, bf16[4,256,256]{2,1,0:T(8,128)(2,1)S(1)}, u32[]{:S(2)}) copy-start(bf16[4,256,256]{2,1,0:T(8,128)(2,1)S(1)} %pad_maximum_fusion) | copy-start | bytes 1572868
  17.5 11.0 %collective-permute-start.4 = (bf16[6,128,256]{2,1,0:T(8,128)(2,1)S(1)}, bf16[6,128,256]{2,1,0:T(8,128)(2,1)S(1)}, u32[]{:S(2)}, u32[]{:S(2)}) collective-permute-start(bf16[6,128,256]{2,1,0:T(8,128)(2,1)S(1)} %broadcast_select_fusion.1), channel_id=1, source_target_pairs={{0,4},{2,6},{4,0},{6,2},{1,5},{3,7},{5,1},{7,3},{8,12},{10,14},{12... | collective-permute-start | bytes 1179656 | tf_op jit(solution)/shard_map/ppermute | solution.py:194
  19.8 12.0 %collective-permute-start.5 = (bf16[6,128,256]{2,1,0:T(8,128)(2,1)S(1)}, bf16[6,128,256]{2,1,0:T(8,128)(2,1)S(1)}, u32[]{:S(2)}, u32[]{:S(2)}) collective-permute-start(bf16[6,128,256]{2,1,0:T(8,128)(2,1)S(1)} %broadcast_select_fusion), channel_id=1, source_target_pairs={{0,6},{2,0},{4,2},{6,4},{1,7},{3,1},{5,3},{7,5},{8,14},{10,8},{12,... | collective-permute-start | bytes 1179656 | tf_op jit(solution)/shard_map/ppermute | solution.py:194
  21.9 16.9 %collective-permute-start.3 = (bf16[6,128,256]{2,1,0:T(8,128)(2,1)S(1)}, bf16[6,128,256]{2,1,0:T(8,128)(2,1)S(1)}, u32[]{:S(2)}, u32[]{:S(2)}) collective-permute-start(bf16[6,128,256]{2,1,0:T(8,128)(2,1)S(1)} %broadcast_select_fusion.2), channel_id=1, source_target_pairs={{0,2},{2,4},{4,6},{6,0},{1,3},{3,5},{5,7},{7,1},{8,10},{10,12},{12... | collective-permute-start | bytes 1179656 | tf_op jit(solution)/shard_map/ppermute | solution.py:194
  28.5 10.4 %copy-start.3 = (bf16[6,128,256]{2,1,0:T(8,128)(2,1)}, bf16[6,128,256]{2,1,0:T(8,128)(2,1)S(1)}, u32[]{:S(2)}) copy-start(bf16[6,128,256]{2,1,0:T(8,128)(2,1)S(1)} %collective-permute-done.4) | copy-start | bytes 1179652
  31.8 7.1 %copy-start.4 = (bf16[6,128,256]{2,1,0:T(8,128)(2,1)}, bf16[6,128,256]{2,1,0:T(8,128)(2,1)S(1)}, u32[]{:S(2)}) copy-start(bf16[6,128,256]{2,1,0:T(8,128)(2,1)S(1)} %collective-permute-done.5) | copy-start | bytes 1179652
  38.9 0.7 copy-start.5
  53.5 29.7 %collective-permute-start.7 = (bf16[6,128,256]{2,1,0:T(8,128)(2,1)S(1)}, bf16[6,128,256]{2,1,0:T(8,128)(2,1)S(1)}, u32[]{:S(2)}, u32[]{:S(2)}) collective-permute-start(bf16[6,128,256]{2,1,0:T(8,128)(2,1)S(1)} %select_convert_fusion.1), channel_id=1, source_target_pairs={{0,4},{2,6},{4,0},{6,2},{1,5},{3,7},{5,1},{7,3},{8,12},{10,14},{12... | collective-permute-start | bytes 1179656 | tf_op jit(solution)/shard_map/ppermute | solution.py:194
  67.4 16.3 %collective-permute-start.6 = (bf16[6,128,256]{2,1,0:T(8,128)(2,1)S(1)}, bf16[6,128,256]{2,1,0:T(8,128)(2,1)S(1)}, u32[]{:S(2)}, u32[]{:S(2)}) collective-permute-start(bf16[6,128,256]{2,1,0:T(8,128)(2,1)S(1)} %select_convert_fusion.2), channel_id=1, source_target_pairs={{0,2},{2,4},{4,6},{6,0},{1,3},{3,5},{5,7},{7,1},{8,10},{10,12},{12... | collective-permute-start | bytes 1179656 | tf_op jit(solution)/shard_map/ppermute | solution.py:194
  69.9 15.4 %collective-permute-start.8 = (bf16[6,128,256]{2,1,0:T(8,128)(2,1)}, bf16[6,128,256]{2,1,0:T(8,128)(2,1)S(1)}, u32[]{:S(2)}, u32[]{:S(2)}) collective-permute-start(bf16[6,128,256]{2,1,0:T(8,128)(2,1)} %select_convert_fusion), channel_id=1, source_target_pairs={{0,6},{2,0},{4,2},{6,4},{1,7},{3,1},{5,3},{7,5},{8,14},{10,8},{12,... | collective-permute-start | bytes 1179656 | tf_op jit(solution)/shard_map/ppermute | solution.py:194
  88.5 10.0 %collective-permute-start.10 = (bf16[2,128,256]{2,1,0:T(8,128)(2,1)S(1)}, bf16[2,128,256]{2,1,0:T(8,128)(2,1)S(1)}, u32[]{:S(2)}, u32[]{:S(2)}) collective-permute-start(bf16[2,128,256]{2,1,0:T(8,128)(2,1)S(1)} %get-tuple-element.37), channel_id=1, source_target_pairs={{0,16},{8,24},{16,0},{24,8},{1,17},{9,25},{17,1},{25,9},{2,18},{10... | collective-permute-start | bytes 393224 | tf_op jit(solution)/shard_map/ppermute | solution.py:194
  88.5 9.9 %collective-permute-start.11 = (bf16[2,128,256]{2,1,0:T(8,128)(2,1)S(1)}, bf16[2,128,256]{2,1,0:T(8,128)(2,1)S(1)}, u32[]{:S(2)}, u32[]{:S(2)}) collective-permute-start(bf16[2,128,256]{2,1,0:T(8,128)(2,1)S(1)} %get-tuple-element.36), channel_id=1, source_target_pairs={{0,24},{8,0},{16,8},{24,16},{1,25},{9,1},{17,9},{25,17},{2,26},{10... | collective-permute-start | bytes 393224 | tf_op jit(solution)/shard_map/ppermute | solution.py:194
  92.9 7.3 %collective-permute-start.9 = (bf16[2,128,256]{2,1,0:T(8,128)(2,1)S(1)}, bf16[2,128,256]{2,1,0:T(8,128)(2,1)S(1)}, u32[]{:S(2)}, u32[]{:S(2)}) collective-permute-start(bf16[2,128,256]{2,1,0:T(8,128)(2,1)S(1)} %get-tuple-element.35), channel_id=1, source_target_pairs={{0,8},{8,16},{16,24},{24,0},{1,9},{9,17},{17,25},{25,1},{2,10},{10... | collective-permute-start | bytes 393224 | tf_op jit(solution)/shard_map/ppermute | solution.py:194
